TPU v7x, 32 devices: a whole 2x2x4 slice. The times are simulated.
32 devices in a mesh: ctx: 8 (over z, x), tp: 4 (over y, core).
Axes of the slice: x: 2, y: 2, z: 4, core: 2. Of those that a mesh axis runs over, the one named last changes fastest.
Arguments:
- tokens: bfloat16 [2048, 16384], P('ctx', 'tp')
- document: int32 [2048], P('ctx'), may hold values from 0 to 5, as said below
- place: int32 [2048], P('ctx'), may hold values from 0 to 1023, as said below
- w_qkv: bfloat16 [1280, 16384], P(None, 'tp')
- w_out: bfloat16 [1024, 16384], P(None, 'tp'), may hold values from -0.1875 to 0.1875
- grad_out: bfloat16 [2048, 16384], P('ctx', 'tp'), may hold values from -6 to 6
Outputs:
- out: bfloat16 [2048, 16384], P('ctx', 'tp')
- grad_x: bfloat16 [2048, 16384], P('ctx', 'tp')
- grad_w_qkv: float32 [1280, 16384], P('ctx', 'tp')
- grad_w_out: float32 [1024, 16384], P('ctx', 'tp')
Inputs may be any that keep to these rules, and one draw needn't show every extreme that they name: Each document's tokens carry the positions 0 to its length minus 1, each once; one document holds 1024 tokens. `place`: position of a token within its document, as described for document.
All inputs are finite; a program needn't handle non-finite values.
Results may differ from a plain program's by a relative error of at most 0.028.
Values may be sent and summed in bfloat16 or wider, within the bound.
No kernel may reach another device: no remote copies, remote signals or barrier semaphores. Data moves between devices by JAX's collectives and lax.ppermute only.
A program may use at most 128 MiB of HBM per device.

v0:
```python
import functools
import math
import jax
import jax.numpy as jnp
from jax import lax
from jax.sharding import PartitionSpec as P

HD = 128
HQ = 8
THETA = 500000.0
NEG = -1e30
PIECE = 64


def angles(place, width):
    half = width // 2
    freq = THETA ** (-(jnp.arange(half, dtype=jnp.float32) * 2.0 / width))
    turn = place.astype(jnp.float32)[:, None] * freq[None, :]
    return (jnp.cos(turn), jnp.sin(turn))


def rotate(vector, cosine, sine):
    half = vector.shape[-1] // 2
    first = vector[..., :half]
    second = vector[..., half:]
    return jnp.concatenate(
        [first * cosine - second * sine, second * cosine + first * sine], axis=-1
    )


def against(left, right):
    return lax.dot_general(
        left, right, (((1,), (1,)), ((), ())), preferred_element_type=jnp.float32
    )


def across(left, right):
    return lax.dot_general(
        left, right, (((0,), (0,)), ((), ())), preferred_element_type=jnp.float32
    )


def ring_of(mesh):
    count = mesh.shape["ctx"]
    try:
        grid = mesh.devices.reshape(count, -1)
        coords = [tuple(grid[i, 0].coords) for i in range(count)]
    except Exception:
        return list(range(count))
    varying = [d for d in range(len(coords[0])) if len({c[d] for c in coords}) > 1]
    if len(varying) == 1:
        return sorted(range(count), key=lambda i: coords[i][varying[0]])
    if len(varying) != 2:
        return list(range(count))
    for short, long in (varying, varying[::-1]):
        levels = sorted({c[short] for c in coords})
        if len(levels) == 2:
            there = sorted(
                (i for i in range(count) if coords[i][short] == levels[0]),
                key=lambda i: coords[i][long],
            )
            back = sorted(
                (i for i in range(count) if coords[i][short] == levels[1]),
                key=lambda i: -coords[i][long],
            )
            return there + back
    return list(range(count))


def ring_scatter(partial, ring, axis):
    count = len(ring)
    where = [0] * count
    for spot, member in enumerate(ring):
        where[member] = spot
    spot = jnp.asarray(where, jnp.int32)[lax.axis_index(axis)]
    order = jnp.asarray(ring, jnp.int32)
    rows = partial.shape[0] // count
    half = partial.shape[1] // 2
    blocks = partial.reshape(count, rows, partial.shape[1])
    left = blocks[:, :, :half]
    right = blocks[:, :, half:]

    def block(side, offset):
        return lax.dynamic_index_in_dim(side, order[(spot + offset) % count], 0, keepdims=False)

    forward = [(ring[p], ring[(p + 1) % count]) for p in range(count)]
    backward = [(ring[p], ring[(p - 1) % count]) for p in range(count)]
    send_left = block(left, count - 1)
    send_right = block(right, 1)
    for step in range(count - 1):
        got_left = lax.ppermute(send_left.astype(jnp.bfloat16), axis, forward)
        got_right = lax.ppermute(send_right.astype(jnp.bfloat16), axis, backward)
        send_left = got_left.astype(jnp.float32) + block(left, 2 * count - step - 2)
        send_right = got_right.astype(jnp.float32) + block(right, step + 2)
    return jnp.concatenate([send_left, send_right], axis=1)


def ring_spot(ring, axis):
    where = [0] * len(ring)
    for spot, member in enumerate(ring):
        where[member] = spot
    return jnp.asarray(where, jnp.int32)[lax.axis_index(axis)]


def ring_gather(value, ring, axis):
    count = len(ring)
    forward = [(ring[p], ring[(p + 1) % count]) for p in range(count)]
    backward = [(ring[p], ring[(p - 1) % count]) for p in range(count)]
    ahead = count // 2
    behind = count - 1 - ahead
    got = [value] + [None] * (count - 1)
    from_left = value
    from_right = value
    for step in range(max(ahead, behind)):
        if step < ahead:
            from_left = lax.ppermute(from_left, axis, forward)
            got[count - step - 1] = from_left
        if step < behind:
            from_right = lax.ppermute(from_right, axis, backward)
            got[step + 1] = from_right
    return jnp.stack(got, axis=0)


def ring_scatter_relative(partial, ring, axis):
    count = len(ring)
    rows = partial.shape[0] // count
    half = partial.shape[1] // 2
    blocks = partial.reshape(count, rows, partial.shape[1])
    left = blocks[:, :, :half]
    right = blocks[:, :, half:]
    forward = [(ring[p], ring[(p + 1) % count]) for p in range(count)]
    backward = [(ring[p], ring[(p - 1) % count]) for p in range(count)]
    send_left = left[count - 1]
    send_right = right[1 % count]
    for step in range(count - 1):
        got_left = lax.ppermute(send_left.astype(jnp.bfloat16), axis, forward)
        got_right = lax.ppermute(send_right.astype(jnp.bfloat16), axis, backward)
        send_left = got_left.astype(jnp.float32) + left[(2 * count - step - 2) % count]
        send_right = got_right.astype(jnp.float32) + right[(step + 2) % count]
    return jnp.concatenate([send_left, send_right], axis=1)


class Ring:

    def __init__(self, partial, ring, axis):
        count = len(ring)
        self.count = count
        self.axis = axis
        self.spot = ring_spot(ring, axis)
        self.order = jnp.asarray(ring, jnp.int32)
        rows = partial.shape[0] // count
        half = partial.shape[1] // 2
        blocks = partial.reshape(count, rows, partial.shape[1])
        self.left = blocks[:, :, :half]
        self.right = blocks[:, :, half:]
        self.forward = [(ring[p], ring[(p + 1) % count]) for p in range(count)]
        self.backward = [(ring[p], ring[(p - 1) % count]) for p in range(count)]
        self.state = (self.block(self.left, count - 1), self.block(self.right, 1))
        self.done = 0

    def block(self, side, offset):
        index = self.order[(self.spot + offset) % self.count]
        return lax.dynamic_index_in_dim(side, index, 0, keepdims=False)

    def advance(self, upto):
        count = self.count
        send_left, send_right = self.state
        for step in range(self.done, min(upto, count - 1)):
            got_left = lax.ppermute(send_left.astype(jnp.bfloat16), self.axis, self.forward)
            got_right = lax.ppermute(send_right.astype(jnp.bfloat16), self.axis, self.backward)
            send_left = got_left.astype(jnp.float32) + self.block(self.left, 2 * count - step - 2)
            send_right = got_right.astype(jnp.float32) + self.block(self.right, step + 2)
            self.done = step + 1
        self.state = (send_left, send_right)
        return self

    def result(self):
        self.advance(self.count - 1)
        return jnp.concatenate(list(self.state), axis=1)


def tp_project(partial, rows_mine, split, axis):
    rank = lax.axis_index(axis)
    core = rank % 2
    near = [(i, i ^ 1) for i in range(4)]
    far = [(i, i ^ 2) for i in range(4)]
    chip = partial + lax.ppermute(partial, axis, near)
    head = chip[:, :split]
    tail = chip[:, split:]
    half_rows = tail.shape[0] // 2
    mine = lax.dynamic_slice_in_dim(head, rank * rows_mine, rows_mine, 0)
    theirs = lax.dynamic_slice_in_dim(head, (rank ^ 2) * rows_mine, rows_mine, 0)
    own_head = mine + lax.ppermute(theirs, axis, far)
    tail_half = lax.dynamic_slice_in_dim(tail, core * half_rows, half_rows, 0)
    tail_half = tail_half + lax.ppermute(tail_half, axis, far)
    other_half = lax.ppermute(tail_half, axis, near)
    first = jnp.where(core == 0, tail_half, other_half)
    second = jnp.where(core == 0, other_half, tail_half)
    return (own_head, jnp.concatenate([first, second], axis=0))


def tp_scatter(partial, rows_mine, axis):
    rank = lax.axis_index(axis)
    far = [(i, i ^ 2) for i in range(4)]
    near = [(i, i ^ 1) for i in range(4)]
    pair_rows = 2 * rows_mine
    chip = rank // 2
    kept = lax.dynamic_slice_in_dim(partial, chip * pair_rows, pair_rows, 0)
    sent = lax.dynamic_slice_in_dim(partial, (1 - chip) * pair_rows, pair_rows, 0)
    kept = kept.astype(jnp.float32) + lax.ppermute(sent.astype(jnp.bfloat16), axis, far).astype(
        jnp.float32
    )
    core = rank % 2
    mine = lax.dynamic_slice_in_dim(kept, core * rows_mine, rows_mine, 0)
    other = lax.dynamic_slice_in_dim(kept, (1 - core) * rows_mine, rows_mine, 0)
    return mine + lax.ppermute(other.astype(jnp.bfloat16), axis, near).astype(jnp.float32)


def direct_gather(value, axis):
    count = lax.axis_size(axis)
    got = [value] + [None] * (count - 1)
    for shift in range(1, count):
        pairs = [(i, (i + shift) % count) for i in range(count)]
        got[count - shift] = lax.ppermute(value, axis, pairs)
    return jnp.stack(got, axis=0)


def direct_scatter(partial, axis):
    count = lax.axis_size(axis)
    rows = partial.shape[0] // count
    blocks = partial.reshape(count, rows, partial.shape[1])
    total = blocks[0]
    for shift in range(1, count):
        pairs = [(i, (i + shift) % count) for i in range(count)]
        total = total + lax.ppermute(blocks[shift].astype(jnp.bfloat16), axis, pairs).astype(
            jnp.float32
        )
    return total


def butterfly_sum(value, axis):
    count = lax.axis_size(axis)
    stride = 1
    while stride < count:
        pairs = [(i, i ^ stride) for i in range(count)]
        value = value + lax.ppermute(value, axis, pairs)
        stride *= 2
    return value


def shards(ring, tokens, document, place, w_qkv, w_out, grad_out):
    rows_ctx, slice_width = tokens.shape
    ctx_size = lax.axis_size("ctx")
    tp_size = lax.axis_size("tp")
    rows_mine = rows_ctx // tp_size
    tp_rank = lax.axis_index("tp")
    head_dim = HD
    heads = HQ
    heads_width = heads * head_dim
    pair_width = 2 * head_dim
    factor = 1.0 / math.sqrt(head_dim)
    first_row = tp_rank * rows_mine
    stacked = heads * rows_mine
    total_rows = ctx_size * rows_ctx
    grad_part = against(grad_out, w_out).astype(jnp.bfloat16)
    cosine_all, sine_all = angles(place, head_dim)
    cosine_mine = lax.dynamic_slice_in_dim(cosine_all, first_row, rows_mine, 0)
    sine_mine = lax.dynamic_slice_in_dim(sine_all, first_row, rows_mine, 0)
    query_doc = lax.dynamic_slice_in_dim(document, first_row, rows_mine, 0)
    query_place = lax.dynamic_slice_in_dim(place, first_row, rows_mine, 0)
    projected = against(tokens, w_qkv)
    if tp_size == 4 and rows_ctx % (2 * tp_size) == 0:
        query_block, pair_rows = tp_project(projected, rows_mine, heads_width, "tp")
    else:
        qkv = lax.psum(projected, "tp")
        query_block = lax.dynamic_slice_in_dim(qkv[:, :heads_width], first_row, rows_mine, 0)
        pair_rows = qkv[:, heads_width:]
    keys = rotate(pair_rows[:, :head_dim], cosine_all, sine_all).astype(jnp.bfloat16)
    values = pair_rows[:, head_dim:].astype(jnp.bfloat16)
    info = jnp.concatenate([document, place // PIECE, place % PIECE], axis=0).astype(jnp.float32)
    info_rows = -(-info.shape[0] // pair_width)
    info = jnp.pad(info, (0, info_rows * pair_width - info.shape[0]))
    info = info.reshape(info_rows, pair_width).astype(jnp.bfloat16)
    packed = jnp.concatenate([keys, values], axis=1)
    packed = jnp.concatenate([packed, info], axis=0)
    gathered = direct_gather(packed, "ctx")
    if tp_size == 4 and rows_ctx % (2 * tp_size) == 0:
        grad_rows = tp_scatter(grad_part, rows_mine, "tp").astype(jnp.bfloat16)
    else:
        grad_rows = lax.psum_scatter(grad_part, "tp", scatter_dimension=0, tiled=True)
    keys_all = gathered[:, :rows_ctx, :head_dim].reshape(total_rows, head_dim)
    values_all = gathered[:, :rows_ctx, head_dim:].reshape(total_rows, head_dim)
    info_all = (
        gathered[:, rows_ctx:, :].reshape(ctx_size, info_rows * pair_width).astype(jnp.float32)
    )
    key_doc = info_all[:, :rows_ctx].reshape(total_rows)
    key_place = (
        info_all[:, rows_ctx : 2 * rows_ctx] * PIECE + info_all[:, 2 * rows_ctx : 3 * rows_ctx]
    ).reshape(total_rows)
    allowed = (query_doc.astype(jnp.float32)[:, None] == key_doc[None, :]) & (
        key_place[None, :] <= query_place.astype(jnp.float32)[:, None]
    )
    allowed = jnp.broadcast_to(allowed[None], (heads, rows_mine, total_rows)).reshape(
        stacked, total_rows
    )
    raw_query = query_block.reshape(rows_mine, heads, head_dim)
    rotated = rotate(raw_query, cosine_mine[:, None, :], sine_mine[:, None, :]).astype(jnp.bfloat16)
    queries = jnp.transpose(rotated, (1, 0, 2)).reshape(stacked, head_dim)
    scores = against(queries, keys_all) * factor
    masked = jnp.where(allowed, scores, NEG)
    top = jnp.max(masked, axis=1)
    weights = jnp.where(allowed, jnp.exp(masked - top[:, None]), 0.0)
    total = jnp.sum(weights, axis=1)
    summed = jnp.dot(weights.astype(jnp.bfloat16), values_all, preferred_element_type=jnp.float32)
    attended = (summed / total[:, None]).astype(jnp.bfloat16)
    logsum = top + jnp.log(total)
    rows_attended = jnp.transpose(attended.reshape(heads, rows_mine, head_dim), (1, 0, 2)).reshape(
        rows_mine, heads_width
    )
    piece = lax.all_gather(rows_attended, "tp", axis=0, tiled=True)
    out = jnp.dot(piece, w_out, preferred_element_type=jnp.float32).astype(jnp.bfloat16)
    out_weight_grad = across(piece, grad_out)
    grad_stack = jnp.transpose(grad_rows.reshape(rows_mine, heads, head_dim), (1, 0, 2)).reshape(
        stacked, head_dim
    )
    delta = jnp.sum(grad_stack.astype(jnp.float32) * attended.astype(jnp.float32), axis=1)
    prob = jnp.where(allowed, jnp.exp(scores - logsum[:, None]), 0.0)
    dprob = against(grad_stack, values_all)
    dscore = (prob * (dprob - delta[:, None])).astype(jnp.bfloat16)
    query_sum = jnp.dot(dscore, keys_all, preferred_element_type=jnp.float32)
    key_part = across(dscore, queries) * factor
    value_part = across(prob.astype(jnp.bfloat16), grad_stack)
    pair_all = jnp.concatenate([key_part, value_part], axis=1)
    out_ring = Ring(out_weight_grad, ring, "ctx").advance(len(ring) // 4)
    pair_grad = butterfly_sum(direct_scatter(pair_all, "ctx"), "tp")
    out_ring.state, pair_grad = lax.optimization_barrier((out_ring.state, pair_grad))
    key_raw = rotate(pair_grad[:, :head_dim], cosine_all, -sine_all)
    query_grad = jnp.transpose((query_sum * factor).reshape(heads, rows_mine, head_dim), (1, 0, 2))
    query_raw = rotate(query_grad, cosine_mine[:, None, :], -sine_mine[:, None, :]).reshape(
        rows_mine, heads_width
    )
    query_rows = lax.all_gather(query_raw.astype(jnp.bfloat16), "tp", axis=0, tiled=True)
    d_qkv = jnp.concatenate(
        [query_rows, key_raw.astype(jnp.bfloat16), pair_grad[:, head_dim:].astype(jnp.bfloat16)],
        axis=1,
    )
    grad_x = jnp.dot(d_qkv, w_qkv, preferred_element_type=jnp.float32).astype(jnp.bfloat16)
    joint_weight = across(d_qkv, tokens)
    out_ring.advance(len(ring) - 1)
    out_ring.state, joint_weight = lax.optimization_barrier((out_ring.state, joint_weight))
    grad_w_qkv = ring_scatter(joint_weight, ring, "ctx")
    grad_w_out = out_ring.result()
    return (out, grad_x, grad_w_qkv, grad_w_out)


def solution(mesh):
    return jax.shard_map(
        functools.partial(shards, ring_of(mesh)),
        mesh=mesh,
        in_specs=(P("ctx", "tp"), P("ctx"), P("ctx"), P(None, "tp"), P(None, "tp"), P("ctx", "tp")),
        out_specs=(P("ctx", "tp"), P("ctx", "tp"), P("ctx", "tp"), P("ctx", "tp")),
        check_vma=False,
    )
```

profile of v0, /device:TPU:0, one launch (start us, length us, event | category | flops | bytes accessed | tf_op | source)
XLA Modules:
  0.0 346.1 jit_solution(10542800763910754592)
XLA Ops:
  2.2 6.9 %fusion.70 = f32[256,1280]{1,0:T(8,128)S(1)} fusion(bf16[256,4096]{1,0:T(8,128)(2,1)S(1)} %copy-done, bf16[1280,4096]{1,0:T(8,128)(2,1)} %param.13), kind=kOutput, calls=%fused_computation.172 | convolution fusion | flops 2684354560 | bytes 13893632 | tf_op jit(solution)/shard_map/dot_general | solution.py:32
  9.6 6.4 %convolution_convert_fusion.2 = bf16[256,1024]{1,0:T(8,128)(2,1)S(1)} fusion(bf16[256,4096]{1,0:T(8,128)(2,1)} %param.15, bf16[1024,4096]{1,0:T(8,128)(2,1)} %param.14), kind=kOutput, calls=%fused_computation.45 | convolution fusion | flops 2147745792 | bytes 11010048 | tf_op jit(solution)/shard_map/dot_general | solution.py:32
  17.6 2.6 collective-permute-start.11
  37.9 4.2 %collective-permute-done.1 = f32[128,256]{1,0:T(8,128)S(1)} collective-permute-done((f32[128,256]{1,0:T(8,128)S(1)}, f32[128,256]{1,0:T(8,128)S(1)}, u32[]{:S(2)}, u32[]{:S(2)}) %collective-permute-start.1) | collective-permute-done | bytes 131104 | tf_op jit(solution)/shard_map/ppermute | solution.py:195
  44.3 4.6 %collective-permute-start.3 = (bf16[259,256]{1,0:T(8,128)(2,1)S(1)}, bf16[259,256]{1,0:T(8,128)(2,1)S(1)}, u32[]{:S(2)}, u32[]{:S(2)}) collective-permute-start(bf16[259,256]{1,0:T(8,128)(2,1)S(1)} %get-tuple-element.19), channel_id=1, source_target_pairs={{0,28},{4,0},{8,4},{12,8},{16,12},{20,16},{24,20},{28,24},{1,29},{... | collective-permute-start | bytes 397832 | tf_op jit(solution)/shard_map/ppermute | solution.py:224
  49.4 3.0 collective-permute-start.6
  54.2 1.6 collective-permute-start.8
  55.8 1.8 collective-permute-start.9
  58.8 13.5 %collective-permute-done.6 = bf16[259,256]{1,0:T(8,128)(2,1)S(1)} collective-permute-done((bf16[259,256]{1,0:T(8,128)(2,1)S(1)}, bf16[259,256]{1,0:T(8,128)(2,1)S(1)}, u32[]{:S(2)}, u32[]{:S(2)}) %collective-permute-start.6) | collective-permute-done | bytes 132640 | tf_op jit(solution)/shard_map/ppermute | solution.py:224
  83.2 2.8 collective-permute-start.19
  86.0 1.6 collective-permute-start.20
  89.0 6.7 %all_gather.6 = bf16[256,1024]{1,0:T(8,128)(2,1)S(1)} all-gather(bf16[64,1024]{1,0:T(8,128)(2,1)S(1)} %bitcast.244), channel_id=1, replica_groups=mesh['ctx'=8,'tp'=4] {'tp'}, dimensions={0}, use_global_device_ids=true | all-gather | bytes 655360 | tf_op jit(solution)/shard_map/all_gather | solution.py:320
  95.7 2.4 fusion.71
  98.2 6.3 %fusion.65 = (f32[8,128,2048]{2,1,0:T(8,128)}, f32[8,128,2048]{2,1,0:T(8,128)}) fusion(f32[8,128,4096]{2,1,0:T(8,128)S(1)} %bitcast.233), kind=kLoop, calls=%fused_computation.167 | loop fusion | bytes 33554432 | tf_op jit(solution)/shard_map/slice | solution.py:155
  104.5 2.4 collective-permute-start.22
  106.9 2.9 collective-permute-start.23
  109.8 2.1 fusion.31
  114.3 2.1 fusion.30
  123.3 2.5 collective-permute-done.15
  125.8 2.3 fusion.26
  128.4 2.7 collective-permute-done.13
  131.1 2.3 fusion.27
  153.9 1.6 bitcast_add_fusion.24
  160.0 10.3 %collective-permute-done.31 = bf16[128,2048]{1,0:T(8,128)(2,1)S(1)} collective-permute-done((bf16[128,2048]{1,0:T(8,128)(2,1)S(1)}, bf16[128,2048]{1,0:T(8,128)(2,1)S(1)}, u32[]{:S(2)}, u32[]{:S(2)}) %collective-permute-start.31) | collective-permute-done | bytes 524320 | tf_op jit(solution)/shard_map/ppermute | solution.py:170
  175.2 9.0 %collective-permute-done.32 = bf16[128,2048]{1,0:T(8,128)(2,1)S(1)} collective-permute-done((bf16[128,2048]{1,0:T(8,128)(2,1)S(1)}, bf16[128,2048]{1,0:T(8,128)(2,1)S(1)}, u32[]{:S(2)}, u32[]{:S(2)}) %collective-permute-start.32) | collective-permute-done | bytes 524320 | tf_op jit(solution)/shard_map/ppermute | solution.py:170
  185.6 1.8 collective-permute-start.33
  189.5 7.1 %all_gather.7 = bf16[256,1024]{1,0:T(8,128)(2,1)} all-gather(bf16[64,1024]{1,0:T(8,128)(2,1)S(1)} %copy_bitcast_fusion.1), channel_id=1, replica_groups=mesh['ctx'=8,'tp'=4] {'tp'}, dimensions={0}, use_global_device_ids=true | all-gather | bytes 655360 | tf_op jit(solution)/shard_map/all_gather | solution.py:342
  196.6 1.7 collective-permute-done.33
  198.3 2.1 fusion.19
  201.4 2.1 fusion.23
  206.4 7.1 %collective-permute-done.34 = bf16[128,2048]{1,0:T(8,128)(2,1)} collective-permute-done((bf16[128,2048]{1,0:T(8,128)(2,1)}, bf16[128,2048]{1,0:T(8,128)(2,1)}, u32[]{:S(2)}, u32[]{:S(2)}) %collective-permute-start.34) | collective-permute-done | bytes 524320 | tf_op jit(solution)/shard_map/ppermute | solution.py:170
  218.9 2.9 fusion.73
  221.8 5.0 %collective-permute-done.35 = bf16[128,2048]{1,0:T(8,128)(2,1)S(1)} collective-permute-done((bf16[128,2048]{1,0:T(8,128)(2,1)S(1)}, bf16[128,2048]{1,0:T(8,128)(2,1)S(1)}, u32[]{:S(2)}, u32[]{:S(2)}) %collective-permute-start.35) | collective-permute-done | bytes 524320 | tf_op jit(solution)/shard_map/ppermute | solution.py:170
  230.9 8.1 %fusion.64 = (f32[8,160,2048]{2,1,0:T(8,128)}, f32[8,160,2048]{2,1,0:T(8,128)}) fusion(f32[8,160,4096]{2,1,0:T(8,128)S(1)} %bitcast.232), kind=kLoop, calls=%fused_computation.166 | loop fusion | bytes 41943040 | tf_op jit(solution)/shard_map/slice | solution.py:80
  241.4 2.0 fusion.29
  244.4 9.9 %collective-permute-done.36 = bf16[160,2048]{1,0:T(8,128)(2,1)S(1)} collective-permute-done((bf16[160,2048]{1,0:T(8,128)(2,1)S(1)}, bf16[160,2048]{1,0:T(8,128)(2,1)S(1)}, u32[]{:S(2)}, u32[]{:S(2)}) %collective-permute-start.36) | collective-permute-done | bytes 655392 | tf_op jit(solution)/shard_map/ppermute | solution.py:91
  259.4 9.8 %collective-permute-done.37 = bf16[160,2048]{1,0:T(8,128)(2,1)S(1)} collective-permute-done((bf16[160,2048]{1,0:T(8,128)(2,1)S(1)}, bf16[160,2048]{1,0:T(8,128)(2,1)S(1)}, u32[]{:S(2)}, u32[]{:S(2)}) %collective-permute-start.37) | collective-permute-done | bytes 655392 | tf_op jit(solution)/shard_map/ppermute | solution.py:91
  274.1 10.0 %collective-permute-done.38 = bf16[160,2048]{1,0:T(8,128)(2,1)S(1)} collective-permute-done((bf16[160,2048]{1,0:T(8,128)(2,1)S(1)}, bf16[160,2048]{1,0:T(8,128)(2,1)S(1)}, u32[]{:S(2)}, u32[]{:S(2)}) %collective-permute-start.38) | collective-permute-done | bytes 655392 | tf_op jit(solution)/shard_map/ppermute | solution.py:91
  287.3 1.6 collective-permute-start.46
  289.0 10.0 %collective-permute-done.39 = bf16[160,2048]{1,0:T(8,128)(2,1)S(1)} collective-permute-done((bf16[160,2048]{1,0:T(8,128)(2,1)S(1)}, bf16[160,2048]{1,0:T(8,128)(2,1)S(1)}, u32[]{:S(2)}, u32[]{:S(2)}) %collective-permute-start.39) | collective-permute-done | bytes 655392 | tf_op jit(solution)/shard_map/ppermute | solution.py:91
  302.2 1.6 collective-permute-start.47
  303.9 7.8 %convolution_convert_fusion = bf16[256,4096]{1,0:T(8,128)(2,1)} fusion(bf16[256,1024]{1,0:T(8,128)(2,1)S(1)} %all_gather.6, bf16[1024,4096]{1,0:T(8,128)(2,1)} %param.14), kind=kOutput, calls=%fused_computation.3 | convolution fusion | flops 2148532224 | bytes 11010048 | tf_op jit(solution)/shard_map/dot_general | solution.py:321
  311.7 2.0 collective-permute-done.40
  318.5 4.1 %convolution_convert_fusion.1 = bf16[256,4096]{1,0:T(8,128)(2,1)} fusion(bf16[256,1280]{1,0:T(8,128)(2,1)S(1)} %concatenate.45, bf16[1280,4096]{1,0:T(8,128)(2,1)S(1)} %bitcast.251), kind=kOutput, calls=%fused_computation.4 | convolution fusion | flops 2685403136 | bytes 13238272 | tf_op jit(solution)/shard_map/dot_general | solution.py:347
  322.7 7.4 %collective-permute-done.41 = bf16[160,2048]{1,0:T(8,128)(2,1)S(1)} collective-permute-done((bf16[160,2048]{1,0:T(8,128)(2,1)S(1)}, bf16[160,2048]{1,0:T(8,128)(2,1)S(1)}, u32[]{:S(2)}, u32[]{:S(2)}) %collective-permute-start.41) | collective-permute-done | bytes 655392 | tf_op jit(solution)/shard_map/ppermute | solution.py:91
  332.4 1.7 collective-permute-start.49
  335.6 6.8 %collective-permute-done.42 = bf16[160,2048]{1,0:T(8,128)(2,1)S(1)} collective-permute-done((bf16[160,2048]{1,0:T(8,128)(2,1)S(1)}, bf16[160,2048]{1,0:T(8,128)(2,1)S(1)}, u32[]{:S(2)}, u32[]{:S(2)}) %collective-permute-start.42) | collective-permute-done | bytes 655392 | tf_op jit(solution)/shard_map/ppermute | solution.py:91
  344.1 1.7 pad_maximum_fusion
  (197 shorter events, 90.0 us)
Async XLA Ops:
  9.1 25.8 %collective-permute-start = (f32[256,1280]{1,0:T(8,128)S(1)}, f32[256,1280]{1,0:T(8,128)}, u32[]{:S(2)}, u32[]{:S(2)}) collective-permute-start(f32[256,1280]{1,0:T(8,128)S(1)} %fusion.70), channel_id=1, source_target_pairs={{0,1},{1,0},{2,3},{3,2},{4,5},{5,4},{6,7},{7,6},{8,9},{9,8},{10,11... | collective-permute-start | bytes 3932168 | tf_op jit(solution)/shard_map/ppermute | solution.py:187
  17.6 19.0 %collective-permute-start.11 = (bf16[128,1024]{1,0:T(8,128)(2,1)}, bf16[128,1024]{1,0:T(8,128)(2,1)}, u32[]{:S(2)}, u32[]{:S(2)}) collective-permute-start(bf16[128,1024]{1,0:T(8,128)(2,1)} %constant_dynamic-slice_fusion), channel_id=1, source_target_pairs={{0,2},{1,3},{2,0},{3,1},{4,6},{5,7},{6,4},{7,5},{8,10},{9,11},{10,... | collective-permute-start | bytes 786440 | tf_op jit(solution)/shard_map/ppermute | solution.py:210
  36.5 5.7 %collective-permute-start.1 = (f32[128,256]{1,0:T(8,128)S(1)}, f32[128,256]{1,0:T(8,128)S(1)}, u32[]{:S(2)}, u32[]{:S(2)}) collective-permute-start(f32[128,256]{1,0:T(8,128)S(1)} %constant_dynamic-slice_fusion.4), channel_id=1, source_target_pairs={{0,2},{1,3},{2,0},{3,1},{4,6},{5,7},{6,4},{7,5},{8,10},{9,11},{10,... | collective-permute-start | bytes 393224 | tf_op jit(solution)/shard_map/ppermute | solution.py:195
  42.5 10.5 %collective-permute-start.10 = (f32[64,1024]{1,0:T(8,128)S(1)}, f32[64,1024]{1,0:T(8,128)S(1)}, u32[]{:S(2)}, u32[]{:S(2)}) collective-permute-start(f32[64,1024]{1,0:T(8,128)S(1)} %constant_dynamic-slice_fusion.3), channel_id=1, source_target_pairs={{0,2},{1,3},{2,0},{3,1},{4,6},{5,7},{6,4},{7,5},{8,10},{9,11},{10,... | collective-permute-start | bytes 786440 | tf_op jit(solution)/shard_map/ppermute | solution.py:193
  44.3 9.8 %collective-permute-start.3 = (bf16[259,256]{1,0:T(8,128)(2,1)S(1)}, bf16[259,256]{1,0:T(8,128)(2,1)S(1)}, u32[]{:S(2)}, u32[]{:S(2)}) collective-permute-start(bf16[259,256]{1,0:T(8,128)(2,1)S(1)} %get-tuple-element.19), channel_id=1, source_target_pairs={{0,28},{4,0},{8,4},{12,8},{16,12},{20,16},{24,20},{28,24},{1,29},{... | collective-permute-start | bytes 397832 | tf_op jit(solution)/shard_map/ppermute | solution.py:224
  48.9 6.9 %collective-permute-start.4 = (bf16[259,256]{1,0:T(8,128)(2,1)S(1)}, bf16[259,256]{1,0:T(8,128)(2,1)S(1)}, u32[]{:S(2)}, u32[]{:S(2)}) collective-permute-start(bf16[259,256]{1,0:T(8,128)(2,1)S(1)} %get-tuple-element.19), channel_id=1, source_target_pairs={{0,24},{4,28},{8,0},{12,4},{16,8},{20,12},{24,16},{28,20},{1,25},{... | collective-permute-start | bytes 397832 | tf_op jit(solution)/shard_map/ppermute | solution.py:224
  49.4 9.4 %collective-permute-start.5 = (bf16[259,256]{1,0:T(8,128)(2,1)S(1)}, bf16[259,256]{1,0:T(8,128)(2,1)S(1)}, u32[]{:S(2)}, u32[]{:S(2)}) collective-permute-start(bf16[259,256]{1,0:T(8,128)(2,1)S(1)} %get-tuple-element.19), channel_id=1, source_target_pairs={{0,20},{4,24},{8,28},{12,0},{16,4},{20,8},{24,12},{28,16},{1,21},{... | collective-permute-start | bytes 397832 | tf_op jit(solution)/shard_map/ppermute | solution.py:224
  49.4 22.9 %collective-permute-start.6 = (bf16[259,256]{1,0:T(8,128)(2,1)S(1)}, bf16[259,256]{1,0:T(8,128)(2,1)S(1)}, u32[]{:S(2)}, u32[]{:S(2)}) collective-permute-start(bf16[259,256]{1,0:T(8,128)(2,1)S(1)} %get-tuple-element.19), channel_id=1, source_target_pairs={{0,16},{4,20},{8,24},{12,28},{16,0},{20,4},{24,8},{28,12},{1,17},{... | collective-permute-start | bytes 397832 | tf_op jit(solution)/shard_map/ppermute | solution.py:224
  53.0 20.7 %collective-permute-start.7 = (bf16[259,256]{1,0:T(8,128)(2,1)S(1)}, bf16[259,256]{1,0:T(8,128)(2,1)S(1)}, u32[]{:S(2)}, u32[]{:S(2)}) collective-permute-start(bf16[259,256]{1,0:T(8,128)(2,1)S(1)} %get-tuple-element.19), channel_id=1, source_target_pairs={{0,12},{4,16},{8,20},{12,24},{16,28},{20,0},{24,4},{28,8},{1,13},{... | collective-permute-start | bytes 397832 | tf_op jit(solution)/shard_map/ppermute | solution.py:224
  54.2 19.6 %collective-permute-start.8 = (bf16[259,256]{1,0:T(8,128)(2,1)S(1)}, bf16[259,256]{1,0:T(8,128)(2,1)S(1)}, u32[]{:S(2)}, u32[]{:S(2)}) collective-permute-start(bf16[259,256]{1,0:T(8,128)(2,1)S(1)} %get-tuple-element.19), channel_id=1, source_target_pairs={{0,8},{4,12},{8,16},{12,20},{16,24},{20,28},{24,0},{28,4},{1,9},{5... | collective-permute-start | bytes 397832 | tf_op jit(solution)/shard_map/ppermute | solution.py:224
  55.8 17.9 %collective-permute-start.9 = (bf16[259,256]{1,0:T(8,128)(2,1)S(1)}, bf16[259,256]{1,0:T(8,128)(2,1)S(1)}, u32[]{:S(2)}, u32[]{:S(2)}) collective-permute-start(bf16[259,256]{1,0:T(8,128)(2,1)S(1)} %get-tuple-element.19), channel_id=1, source_target_pairs={{0,4},{4,8},{8,12},{12,16},{16,20},{20,24},{24,28},{28,0},{1,5},{5... | collective-permute-start | bytes 397832 | tf_op jit(solution)/shard_map/ppermute | solution.py:224
  82.3 22.2 %collective-permute-start.17 = (bf16[256,256]{1,0:T(8,128)(2,1)}, bf16[256,256]{1,0:T(8,128)(2,1)}, u32[]{:S(2)}, u32[]{:S(2)}) collective-permute-start(bf16[256,256]{1,0:T(8,128)(2,1)} %get-tuple-element.30), channel_id=1, source_target_pairs={{0,4},{4,8},{8,12},{12,16},{16,20},{20,24},{24,28},{28,0},{1,5},{5... | collective-permute-start | bytes 393224 | tf_op jit(solution)/shard_map/ppermute | solution.py:235
  82.3 24.6 %collective-permute-start.18 = (bf16[256,256]{1,0:T(8,128)(2,1)}, bf16[256,256]{1,0:T(8,128)(2,1)}, u32[]{:S(2)}, u32[]{:S(2)}) collective-permute-start(bf16[256,256]{1,0:T(8,128)(2,1)} %get-tuple-element.36), channel_id=1, source_target_pairs={{0,8},{4,12},{8,16},{12,20},{16,24},{20,28},{24,0},{28,4},{1,9},{5... | collective-permute-start | bytes 393224 | tf_op jit(solution)/shard_map/ppermute | solution.py:235
  83.2 28.7 %collective-permute-start.19 = (bf16[256,256]{1,0:T(8,128)(2,1)}, bf16[256,256]{1,0:T(8,128)(2,1)}, u32[]{:S(2)}, u32[]{:S(2)}) collective-permute-start(bf16[256,256]{1,0:T(8,128)(2,1)} %get-tuple-element.35), channel_id=1, source_target_pairs={{0,12},{4,16},{8,20},{12,24},{16,28},{20,0},{24,4},{28,8},{1,13},{... | collective-permute-start | bytes 393224 | tf_op jit(solution)/shard_map/ppermute | solution.py:235
  86.0 25.9 %collective-permute-start.20 = (bf16[256,256]{1,0:T(8,128)(2,1)}, bf16[256,256]{1,0:T(8,128)(2,1)}, u32[]{:S(2)}, u32[]{:S(2)}) collective-permute-start(bf16[256,256]{1,0:T(8,128)(2,1)} %get-tuple-element.34), channel_id=1, source_target_pairs={{0,16},{4,20},{8,24},{12,28},{16,0},{20,4},{24,8},{28,12},{1,17},{... | collective-permute-start | bytes 393224 | tf_op jit(solution)/shard_map/ppermute | solution.py:235
  87.6 24.3 %collective-permute-start.21 = (bf16[256,256]{1,0:T(8,128)(2,1)}, bf16[256,256]{1,0:T(8,128)(2,1)}, u32[]{:S(2)}, u32[]{:S(2)}) collective-permute-start(bf16[256,256]{1,0:T(8,128)(2,1)} %get-tuple-element.33), channel_id=1, source_target_pairs={{0,20},{4,24},{8,28},{12,0},{16,4},{20,8},{24,12},{28,16},{1,21},{... | collective-permute-start | bytes 393224 | tf_op jit(solution)/shard_map/ppermute | solution.py:235
  104.5 7.4 %collective-permute-start.22 = (bf16[256,256]{1,0:T(8,128)(2,1)S(1)}, bf16[256,256]{1,0:T(8,128)(2,1)S(1)}, u32[]{:S(2)}, u32[]{:S(2)}) collective-permute-start(bf16[256,256]{1,0:T(8,128)(2,1)S(1)} %get-tuple-element.32), channel_id=1, source_target_pairs={{0,24},{4,28},{8,0},{12,4},{16,8},{20,12},{24,16},{28,20},{1,25},{... | collective-permute-start | bytes 393224 | tf_op jit(solution)/shard_map/ppermute | solution.py:235
  106.9 6.1 %collective-permute-start.23 = (bf16[256,256]{1,0:T(8,128)(2,1)S(1)}, bf16[256,256]{1,0:T(8,128)(2,1)S(1)}, u32[]{:S(2)}, u32[]{:S(2)}) collective-permute-start(bf16[256,256]{1,0:T(8,128)(2,1)S(1)} %get-tuple-element.31), channel_id=1, source_target_pairs={{0,28},{4,0},{8,4},{12,8},{16,12},{20,16},{24,20},{28,24},{1,29},{... | collective-permute-start | bytes 393224 | tf_op jit(solution)/shard_map/ppermute | solution.py:235
  111.9 13.9 %collective-permute-start.15 = (bf16[128,2048]{1,0:T(8,128)(2,1)}, bf16[128,2048]{1,0:T(8,128)(2,1)}, u32[]{:S(2)}, u32[]{:S(2)}) collective-permute-start(bf16[128,2048]{1,0:T(8,128)(2,1)} %fusion.31), channel_id=1, source_target_pairs={{0,4},{8,0},{16,8},{24,16},{28,24},{20,28},{12,20},{4,12},{1,5},{9... | collective-permute-start | bytes 1572872 | tf_op jit(solution)/shard_map/ppermute | solution.py:170
  114.2 7.0 %collective-permute-start.24 = (f32[256,256]{1,0:T(8,128)S(1)}, f32[256,256]{1,0:T(8,128)}, u32[]{:S(2)}, u32[]{:S(2)}) collective-permute-start(f32[256,256]{1,0:T(8,128)S(1)} %fusion.39), channel_id=1, source_target_pairs={{0,1},{1,0},{2,3},{3,2},{4,5},{5,4},{6,7},{7,6},{8,9},{9,8},{10,11... | collective-permute-start | bytes 786440 | tf_op jit(solution)/shard_map/ppermute | solution.py:246
  116.4 14.6 %collective-permute-start.13 = (bf16[128,2048]{1,0:T(8,128)(2,1)}, bf16[128,2048]{1,0:T(8,128)(2,1)}, u32[]{:S(2)}, u32[]{:S(2)}) collective-permute-start(bf16[128,2048]{1,0:T(8,128)(2,1)} %fusion.30), channel_id=1, source_target_pairs={{0,8},{8,16},{16,24},{24,28},{28,20},{20,12},{12,4},{4,0},{1,9},{9... | collective-permute-start | bytes 1572872 | tf_op jit(solution)/shard_map/ppermute | solution.py:169
  122.3 30.6 %collective-permute-start.25 = (f32[256,256]{1,0:T(8,128)S(1)}, f32[256,256]{1,0:T(8,128)}, u32[]{:S(2)}, u32[]{:S(2)}) collective-permute-start(f32[256,256]{1,0:T(8,128)S(1)} %add.689), channel_id=1, source_target_pairs={{0,2},{1,3},{2,0},{3,1},{4,6},{5,7},{6,4},{7,5},{8,10},{9,11},{10,... | collective-permute-start | bytes 786440 | tf_op jit(solution)/shard_map/ppermute | solution.py:246
  128.1 25.8 %collective-permute-start.16 = (bf16[128,2048]{1,0:T(8,128)(2,1)}, bf16[128,2048]{1,0:T(8,128)(2,1)}, u32[]{:S(2)}, u32[]{:S(2)}) collective-permute-start(bf16[128,2048]{1,0:T(8,128)(2,1)} %fusion.26), channel_id=1, source_target_pairs={{0,4},{8,0},{16,8},{24,16},{28,24},{20,28},{12,20},{4,12},{1,5},{9... | collective-permute-start | bytes 1572872 | tf_op jit(solution)/shard_map/ppermute | solution.py:170
  133.3 22.2 %collective-permute-start.14 = (bf16[128,2048]{1,0:T(8,128)(2,1)}, bf16[128,2048]{1,0:T(8,128)(2,1)}, u32[]{:S(2)}, u32[]{:S(2)}) collective-permute-start(bf16[128,2048]{1,0:T(8,128)(2,1)} %fusion.27), channel_id=1, source_target_pairs={{0,8},{8,16},{16,24},{24,28},{28,20},{20,12},{12,4},{4,0},{1,9},{9... | collective-permute-start | bytes 1572872 | tf_op jit(solution)/shard_map/ppermute | solution.py:169
  157.0 13.3 %collective-permute-start.31 = (bf16[128,2048]{1,0:T(8,128)(2,1)S(1)}, bf16[128,2048]{1,0:T(8,128)(2,1)S(1)}, u32[]{:S(2)}, u32[]{:S(2)}) collective-permute-start(bf16[128,2048]{1,0:T(8,128)(2,1)S(1)} %bitcast_add_fusion.24), channel_id=1, source_target_pairs={{0,4},{8,0},{16,8},{24,16},{28,24},{20,28},{12,20},{4,12},{1,5},{9... | collective-permute-start | bytes 1572872 | tf_op jit(solution)/shard_map/ppermute | solution.py:170
  158.8 14.4 %collective-permute-start.26 = (bf16[128,2048]{1,0:T(8,128)(2,1)S(1)}, bf16[128,2048]{1,0:T(8,128)(2,1)S(1)}, u32[]{:S(2)}, u32[]{:S(2)}) collective-permute-start(bf16[128,2048]{1,0:T(8,128)(2,1)S(1)} %bitcast_add_fusion.26), channel_id=1, source_target_pairs={{0,8},{8,16},{16,24},{24,28},{28,20},{20,12},{12,4},{4,0},{1,9},{9... | collective-permute-start | bytes 1572872 | tf_op jit(solution)/shard_map/ppermute | solution.py:169
  171.6 12.6 %collective-permute-start.32 = (bf16[128,2048]{1,0:T(8,128)(2,1)S(1)}, bf16[128,2048]{1,0:T(8,128)(2,1)S(1)}, u32[]{:S(2)}, u32[]{:S(2)}) collective-permute-start(bf16[128,2048]{1,0:T(8,128)(2,1)S(1)} %fusion.21), channel_id=1, source_target_pairs={{0,4},{8,0},{16,8},{24,16},{28,24},{20,28},{12,20},{4,12},{1,5},{9... | collective-permute-start | bytes 1572872 | tf_op jit(solution)/shard_map/ppermute | solution.py:170
  174.5 12.9 %collective-permute-start.27 = (bf16[128,2048]{1,0:T(8,128)(2,1)S(1)}, bf16[128,2048]{1,0:T(8,128)(2,1)S(1)}, u32[]{:S(2)}, u32[]{:S(2)}) collective-permute-start(bf16[128,2048]{1,0:T(8,128)(2,1)S(1)} %fusion.25), channel_id=1, source_target_pairs={{0,8},{8,16},{16,24},{24,28},{28,20},{20,12},{12,4},{4,0},{1,9},{9... | collective-permute-start | bytes 1572872 | tf_op jit(solution)/shard_map/ppermute | solution.py:169
  185.6 12.8 %collective-permute-start.33 = (bf16[128,2048]{1,0:T(8,128)(2,1)S(1)}, bf16[128,2048]{1,0:T(8,128)(2,1)S(1)}, u32[]{:S(2)}, u32[]{:S(2)}) collective-permute-start(bf16[128,2048]{1,0:T(8,128)(2,1)S(1)} %fusion.20), channel_id=1, source_target_pairs={{0,4},{8,0},{16,8},{24,16},{28,24},{20,28},{12,20},{4,12},{1,5},{9... | collective-permute-start | bytes 1572872 | tf_op jit(solution)/shard_map/ppermute | solution.py:170
  188.7 12.7 %collective-permute-start.28 = (bf16[128,2048]{1,0:T(8,128)(2,1)S(1)}, bf16[128,2048]{1,0:T(8,128)(2,1)S(1)}, u32[]{:S(2)}, u32[]{:S(2)}) collective-permute-start(bf16[128,2048]{1,0:T(8,128)(2,1)S(1)} %fusion.24), channel_id=1, source_target_pairs={{0,8},{8,16},{16,24},{24,28},{28,20},{20,12},{12,4},{4,0},{1,9},{9... | collective-permute-start | bytes 1572872 | tf_op jit(solution)/shard_map/ppermute | solution.py:169
  200.5 13.0 %collective-permute-start.34 = (bf16[128,2048]{1,0:T(8,128)(2,1)}, bf16[128,2048]{1,0:T(8,128)(2,1)}, u32[]{:S(2)}, u32[]{:S(2)}) collective-permute-start(bf16[128,2048]{1,0:T(8,128)(2,1)} %fusion.19), channel_id=1, source_target_pairs={{0,4},{8,0},{16,8},{24,16},{28,24},{20,28},{12,20},{4,12},{1,5},{9... | collective-permute-start | bytes 1572872 | tf_op jit(solution)/shard_map/ppermute | solution.py:170
  203.5 12.9 %collective-permute-start.29 = (bf16[128,2048]{1,0:T(8,128)(2,1)}, bf16[128,2048]{1,0:T(8,128)(2,1)}, u32[]{:S(2)}, u32[]{:S(2)}) collective-permute-start(bf16[128,2048]{1,0:T(8,128)(2,1)} %fusion.23), channel_id=1, source_target_pairs={{0,8},{8,16},{16,24},{24,28},{28,20},{20,12},{12,4},{4,0},{1,9},{9... | collective-permute-start | bytes 1572872 | tf_op jit(solution)/shard_map/ppermute | solution.py:169
  215.0 11.9 %collective-permute-start.35 = (bf16[128,2048]{1,0:T(8,128)(2,1)S(1)}, bf16[128,2048]{1,0:T(8,128)(2,1)S(1)}, u32[]{:S(2)}, u32[]{:S(2)}) collective-permute-start(bf16[128,2048]{1,0:T(8,128)(2,1)S(1)} %fusion.18), channel_id=1, source_target_pairs={{0,4},{8,0},{16,8},{24,16},{28,24},{20,28},{12,20},{4,12},{1,5},{9... | collective-permute-start | bytes 1572872 | tf_op jit(solution)/shard_map/ppermute | solution.py:170
  217.8 11.7 %collective-permute-start.30 = (bf16[128,2048]{1,0:T(8,128)(2,1)S(1)}, bf16[128,2048]{1,0:T(8,128)(2,1)S(1)}, u32[]{:S(2)}, u32[]{:S(2)}) collective-permute-start(bf16[128,2048]{1,0:T(8,128)(2,1)S(1)} %fusion.22), channel_id=1, source_target_pairs={{0,8},{8,16},{16,24},{24,28},{28,20},{20,12},{12,4},{4,0},{1,9},{9... | collective-permute-start | bytes 1572872 | tf_op jit(solution)/shard_map/ppermute | solution.py:169
  240.5 13.8 %collective-permute-start.36 = (bf16[160,2048]{1,0:T(8,128)(2,1)S(1)}, bf16[160,2048]{1,0:T(8,128)(2,1)S(1)}, u32[]{:S(2)}, u32[]{:S(2)}) collective-permute-start(bf16[160,2048]{1,0:T(8,128)(2,1)S(1)} %fusion.28), channel_id=1, source_target_pairs={{0,8},{8,16},{16,24},{24,28},{28,20},{20,12},{12,4},{4,0},{1,9},{9... | collective-permute-start | bytes 1966088 | tf_op jit(solution)/shard_map/ppermute | solution.py:91
  243.5 13.5 %collective-permute-start.43 = (bf16[160,2048]{1,0:T(8,128)(2,1)S(1)}, bf16[160,2048]{1,0:T(8,128)(2,1)S(1)}, u32[]{:S(2)}, u32[]{:S(2)}) collective-permute-start(bf16[160,2048]{1,0:T(8,128)(2,1)S(1)} %fusion.29), channel_id=1, source_target_pairs={{0,4},{8,0},{16,8},{24,16},{28,24},{20,28},{12,20},{4,12},{1,5},{9... | collective-permute-start | bytes 1966088 | tf_op jit(solution)/shard_map/ppermute | solution.py:92
  255.8 13.4 %collective-permute-start.37 = (bf16[160,2048]{1,0:T(8,128)(2,1)S(1)}, bf16[160,2048]{1,0:T(8,128)(2,1)S(1)}, u32[]{:S(2)}, u32[]{:S(2)}) collective-permute-start(bf16[160,2048]{1,0:T(8,128)(2,1)S(1)} %fusion.16), channel_id=1, source_target_pairs={{0,8},{8,16},{16,24},{24,28},{28,20},{20,12},{12,4},{4,0},{1,9},{9... | collective-permute-start | bytes 1966088 | tf_op jit(solution)/shard_map/ppermute | solution.py:91
  258.5 13.8 %collective-permute-start.44 = (bf16[160,2048]{1,0:T(8,128)(2,1)S(1)}, bf16[160,2048]{1,0:T(8,128)(2,1)S(1)}, u32[]{:S(2)}, u32[]{:S(2)}) collective-permute-start(bf16[160,2048]{1,0:T(8,128)(2,1)S(1)} %fusion.10), channel_id=1, source_target_pairs={{0,4},{8,0},{16,8},{24,16},{28,24},{20,28},{12,20},{4,12},{1,5},{9... | collective-permute-start | bytes 1966088 | tf_op jit(solution)/shard_map/ppermute | solution.py:92
  270.7 13.4 %collective-permute-start.38 = (bf16[160,2048]{1,0:T(8,128)(2,1)S(1)}, bf16[160,2048]{1,0:T(8,128)(2,1)S(1)}, u32[]{:S(2)}, u32[]{:S(2)}) collective-permute-start(bf16[160,2048]{1,0:T(8,128)(2,1)S(1)} %fusion.15), channel_id=1, source_target_pairs={{0,8},{8,16},{16,24},{24,28},{28,20},{20,12},{12,4},{4,0},{1,9},{9... | collective-permute-start | bytes 1966088 | tf_op jit(solution)/shard_map/ppermute | solution.py:91
  272.5 14.7 %collective-permute-start.45 = (bf16[160,2048]{1,0:T(8,128)(2,1)S(1)}, bf16[160,2048]{1,0:T(8,128)(2,1)S(1)}, u32[]{:S(2)}, u32[]{:S(2)}) collective-permute-start(bf16[160,2048]{1,0:T(8,128)(2,1)S(1)} %fusion.9), channel_id=1, source_target_pairs={{0,4},{8,0},{16,8},{24,16},{28,24},{20,28},{12,20},{4,12},{1,5},{9... | collective-permute-start | bytes 1966088 | tf_op jit(solution)/shard_map/ppermute | solution.py:92
  285.6 13.4 %collective-permute-start.39 = (bf16[160,2048]{1,0:T(8,128)(2,1)S(1)}, bf16[160,2048]{1,0:T(8,128)(2,1)S(1)}, u32[]{:S(2)}, u32[]{:S(2)}) collective-permute-start(bf16[160,2048]{1,0:T(8,128)(2,1)S(1)} %fusion.14), channel_id=1, source_target_pairs={{0,8},{8,16},{16,24},{24,28},{28,20},{20,12},{12,4},{4,0},{1,9},{9... | collective-permute-start | bytes 1966088 | tf_op jit(solution)/shard_map/ppermute | solution.py:91
  287.3 14.7 %collective-permute-start.46 = (bf16[160,2048]{1,0:T(8,128)(2,1)S(1)}, bf16[160,2048]{1,0:T(8,128)(2,1)S(1)}, u32[]{:S(2)}, u32[]{:S(2)}) collective-permute-start(bf16[160,2048]{1,0:T(8,128)(2,1)S(1)} %fusion.8), channel_id=1, source_target_pairs={{0,4},{8,0},{16,8},{24,16},{28,24},{20,28},{12,20},{4,12},{1,5},{9... | collective-permute-start | bytes 1966088 | tf_op jit(solution)/shard_map/ppermute | solution.py:92
  300.5 13.2 %collective-permute-start.40 = (bf16[160,2048]{1,0:T(8,128)(2,1)S(1)}, bf16[160,2048]{1,0:T(8,128)(2,1)S(1)}, u32[]{:S(2)}, u32[]{:S(2)}) collective-permute-start(bf16[160,2048]{1,0:T(8,128)(2,1)S(1)} %fusion.13), channel_id=1, source_target_pairs={{0,8},{8,16},{16,24},{24,28},{28,20},{20,12},{12,4},{4,0},{1,9},{9... | collective-permute-start | bytes 1966088 | tf_op jit(solution)/shard_map/ppermute | solution.py:91
  302.2 14.7 %collective-permute-start.47 = (bf16[160,2048]{1,0:T(8,128)(2,1)S(1)}, bf16[160,2048]{1,0:T(8,128)(2,1)S(1)}, u32[]{:S(2)}, u32[]{:S(2)}) collective-permute-start(bf16[160,2048]{1,0:T(8,128)(2,1)S(1)} %fusion.7), channel_id=1, source_target_pairs={{0,4},{8,0},{16,8},{24,16},{28,24},{20,28},{12,20},{4,12},{1,5},{9... | collective-permute-start | bytes 1966088 | tf_op jit(solution)/shard_map/ppermute | solution.py:92
  315.1 14.9 %collective-permute-start.41 = (bf16[160,2048]{1,0:T(8,128)(2,1)S(1)}, bf16[160,2048]{1,0:T(8,128)(2,1)S(1)}, u32[]{:S(2)}, u32[]{:S(2)}) collective-permute-start(bf16[160,2048]{1,0:T(8,128)(2,1)S(1)} %fusion.12), channel_id=1, source_target_pairs={{0,8},{8,16},{16,24},{24,28},{28,20},{20,12},{12,4},{4,0},{1,9},{9... | collective-permute-start | bytes 1966088 | tf_op jit(solution)/shard_map/ppermute | solution.py:91
  317.1 15.2 %collective-permute-start.48 = (bf16[160,2048]{1,0:T(8,128)(2,1)S(1)}, bf16[160,2048]{1,0:T(8,128)(2,1)S(1)}, u32[]{:S(2)}, u32[]{:S(2)}) collective-permute-start(bf16[160,2048]{1,0:T(8,128)(2,1)S(1)} %fusion.6), channel_id=1, source_target_pairs={{0,4},{8,0},{16,8},{24,16},{28,24},{20,28},{12,20},{4,12},{1,5},{9... | collective-permute-start | bytes 1966088 | tf_op jit(solution)/shard_map/ppermute | solution.py:92
  331.5 10.9 %collective-permute-start.42 = (bf16[160,2048]{1,0:T(8,128)(2,1)S(1)}, bf16[160,2048]{1,0:T(8,128)(2,1)S(1)}, u32[]{:S(2)}, u32[]{:S(2)}) collective-permute-start(bf16[160,2048]{1,0:T(8,128)(2,1)S(1)} %fusion.11), channel_id=1, source_target_pairs={{0,8},{8,16},{16,24},{24,28},{28,20},{20,12},{12,4},{4,0},{1,9},{9... | collective-permute-start | bytes 1966088 | tf_op jit(solution)/shard_map/ppermute | solution.py:91
  332.4 11.5 %collective-permute-start.49 = (bf16[160,2048]{1,0:T(8,128)(2,1)S(1)}, bf16[160,2048]{1,0:T(8,128)(2,1)S(1)}, u32[]{:S(2)}, u32[]{:S(2)}) collective-permute-start(bf16[160,2048]{1,0:T(8,128)(2,1)S(1)} %fusion.5), channel_id=1, source_target_pairs={{0,4},{8,0},{16,8},{24,16},{28,24},{20,28},{12,20},{4,12},{1,5},{9... | collective-permute-start | bytes 1966088 | tf_op jit(solution)/shard_map/ppermute | solution.py:92
  (21 other events, 188.3 us)
where the time goes:
time: 348 us; the launch traced here: 346 us
  waiting for transfers between devices  122 us (35%)
  starting transfers between devices  57.5 us (17%)
  other arithmetic  50 us (14%)
  between operations  37.1 us (11%)
  matrix products  35.2 us (10%)
  local copies, waits for them, and re-layouts  30.3 us (9%)
  blocking collectives  13.8 us (4%)
    ppermute x7, waiting for transfers between devices, ring_scatter(): got_left = lax.ppermute(send_left.astype(jnp.bfloat16), axis, forward)  55.9 us
    ppermute x7, waiting for transfers between devices, advance(): lax.ppermute(send_right.astype(jnp.bfloat16), self.axis, self.backward)  35.6 us
    ppermute x7, waiting for transfers between devices, direct_gather(): got[count - shift] = lax.ppermute(value, axis, pairs)  16.1 us
    dot_general x4, matrix products, against(): lax.dot_general(left, right, (((1,), (1,)), ((), ())), preferred_element_...  14.9 us
    ppermute x7, starting transfers between devices, direct_gather(): got[count - shift] = lax.ppermute(value, axis, pairs)  12.2 us
    ppermute x7, starting transfers between devices, direct_scatter(): lax.ppermute(blocks[shift].astype(jnp.bfloat16), axis, pairs)  11.9 us
    ppermute x7, starting transfers between devices, ring_scatter(): got_right = lax.ppermute(send_right.astype(jnp.bfloat16), axis, backward)  9.87 us
    convert_element_type x6, other arithmetic, ring_scatter(): got_left = lax.ppermute(send_left.astype(jnp.bfloat16), axis, forward)  8.84 us
  transfers between devices with their start and end apart: 50, of which 28 were waited for; matrix products, arithmetic and copies ran while one was open for 24% of the time, Pallas kernels for 0%

commit v1 on v0

--- a/solution.py
+++ b/solution.py
@@ -10,6 +10,34 @@
 THETA = 500000.0
 NEG = -1e30
 PIECE = 64
+
+
+def _update_tasks(chunk, d_out):
+    prior, x_next, spare = (jax.lax.axis_size("tp"), jax.lax.axis_index("tp"), chunk.shape[d_out])
+    found = tuple((ix * prior if hop_no == d_out else ix for hop_no, ix in enumerate(chunk.shape)))
+    r2 = lax.dynamic_update_slice_in_dim(
+        jnp.zeros(found, chunk.dtype), chunk, x_next * spare, axis=d_out
+    )
+    kept_arr = everything = chunk
+    for i0 in range(1, prior // 2 + 1):
+        kept_arr = jax.lax.ppermute(
+            kept_arr,
+            axis_name="tp",
+            perm=tuple(((hop_no, (hop_no + 1) % prior) for hop_no in range(prior))),
+        )
+        r2 = lax.dynamic_update_slice_in_dim(
+            r2, kept_arr, (x_next - i0) % prior * spare, axis=d_out
+        )
+        if 2 * i0 < prior:
+            everything = jax.lax.ppermute(
+                everything,
+                axis_name="tp",
+                perm=tuple(((hop_no, (hop_no - 1) % prior) for hop_no in range(prior))),
+            )
+            r2 = lax.dynamic_update_slice_in_dim(
+                r2, everything, (x_next + i0) % prior * spare, axis=d_out
+            )
+    return r2
 
 
 def angles(place, width):
@@ -339,7 +367,7 @@
     query_raw = rotate(query_grad, cosine_mine[:, None, :], -sine_mine[:, None, :]).reshape(
         rows_mine, heads_width
     )
-    query_rows = lax.all_gather(query_raw.astype(jnp.bfloat16), "tp", axis=0, tiled=True)
+    query_rows = _update_tasks(query_raw.astype(jnp.bfloat16), 0)
     d_qkv = jnp.concatenate(
         [query_rows, key_raw.astype(jnp.bfloat16), pair_grad[:, head_dim:].astype(jnp.bfloat16)],
         axis=1,

time: 348 us -> 360 us (1.034)
  waiting for transfers between devices: 122 us -> 139 us
  blocking collectives: 13.8 us -> 6.7 us
  starting transfers between devices: 57.5 us -> 61.5 us
    ppermute x7, waiting for transfers between devices: 4.4 us -> 49.8 us  [advance(): lax.ppermute(send_left.astype(jnp.bfloat16), self.axis, self.forward)]
    ppermute x7, waiting for transfers between devices: 35.6 us -> 7.26 us  [advance(): lax.ppermute(send_right.astype(jnp.bfloat16), self.axis, self.backward)]
    all_gather x1 -> x0, blocking collectives: 7.11 us -> none  [shards(): lax.all_gather(query_raw.astype(jnp.bfloat16), 'tp', axis=0, tiled=True)]
    ppermute x7, starting transfers between devices: 9.87 us -> 14.2 us  [ring_scatter(): got_right = lax.ppermute(send_right.astype(jnp.bfloat16), axis, backward)]
  transfers between devices with their start and end apart: 50 -> 53, of which waited for: 28 -> 27; matrix products, arithmetic and copies ran while one was open for 24% -> 23% of each run, Pallas kernels for 0% -> 0%
where the time goes in v1:
time: 360 us; the launch traced here: 358 us
  waiting for transfers between devices  139 us (39%)
  starting transfers between devices  61.5 us (17%)
  other arithmetic  49 us (14%)
  between operations  37 us (10%)
  matrix products  35 us (10%)
  local copies, waits for them, and re-layouts  30.2 us (8%)
  blocking collectives  6.7 us (2%)
    ppermute x7, waiting for transfers between devices, ring_scatter(): got_left = lax.ppermute(send_left.astype(jnp.bfloat16), axis, forward)  53.6 us
    ppermute x7, waiting for transfers between devices, advance(): lax.ppermute(send_left.astype(jnp.bfloat16), self.axis, self.forward)  49.8 us
    ppermute x7, waiting for transfers between devices, direct_gather(): got[count - shift] = lax.ppermute(value, axis, pairs)  16.1 us
    dot_general x4, matrix products, against(): lax.dot_general(left, right, (((1,), (1,)), ((), ())), preferred_element_...  14.9 us
    ppermute x7, starting transfers between devices, ring_scatter(): got_right = lax.ppermute(send_right.astype(jnp.bfloat16), axis, backward)  14.2 us
    ppermute x7, starting transfers between devices, direct_gather(): got[count - shift] = lax.ppermute(value, axis, pairs)  12.2 us
    ppermute x7, starting transfers between devices, direct_scatter(): lax.ppermute(blocks[shift].astype(jnp.bfloat16), axis, pairs)  11.9 us
    ppermute x7, starting transfers between devices, advance(): lax.ppermute(send_right.astype(jnp.bfloat16), self.axis, self.backward)  9.95 us
  transfers between devices with their start and end apart: 53, of which 27 were waited for; matrix products, arithmetic and copies ran while one was open for 23% of the time, Pallas kernels for 0%

profile of v1, /device:TPU:0, one launch (start us, length us, event | category | flops | bytes accessed | tf_op | source)
XLA Modules:
  0.0 358.3 jit_solution(13837964466086303119)
XLA Ops:
  2.2 6.9 %fusion.70 = f32[256,1280]{1,0:T(8,128)S(1)} fusion(bf16[256,4096]{1,0:T(8,128)(2,1)S(1)} %copy-done, bf16[1280,4096]{1,0:T(8,128)(2,1)} %param.13), kind=kOutput, calls=%fused_computation.176 | convolution fusion | flops 2684354560 | bytes 13893632 | tf_op jit(solution)/shard_map/dot_general | solution.py:60
  9.6 6.4 %convolution_convert_fusion.2 = bf16[256,1024]{1,0:T(8,128)(2,1)S(1)} fusion(bf16[256,4096]{1,0:T(8,128)(2,1)} %param.15, bf16[1024,4096]{1,0:T(8,128)(2,1)} %param.14), kind=kOutput, calls=%fused_computation.45 | convolution fusion | flops 2147745792 | bytes 11010048 | tf_op jit(solution)/shard_map/dot_general | solution.py:60
  17.6 2.6 collective-permute-start.11
  37.9 4.2 %collective-permute-done.1 = f32[128,256]{1,0:T(8,128)S(1)} collective-permute-done((f32[128,256]{1,0:T(8,128)S(1)}, f32[128,256]{1,0:T(8,128)S(1)}, u32[]{:S(2)}, u32[]{:S(2)}) %collective-permute-start.1) | collective-permute-done | bytes 131104 | tf_op jit(solution)/shard_map/ppermute | solution.py:223
  44.3 4.6 %collective-permute-start.3 = (bf16[259,256]{1,0:T(8,128)(2,1)S(1)}, bf16[259,256]{1,0:T(8,128)(2,1)S(1)}, u32[]{:S(2)}, u32[]{:S(2)}) collective-permute-start(bf16[259,256]{1,0:T(8,128)(2,1)S(1)} %get-tuple-element.19), channel_id=1, source_target_pairs={{0,28},{4,0},{8,4},{12,8},{16,12},{20,16},{24,20},{28,24},{1,29},{... | collective-permute-start | bytes 397832 | tf_op jit(solution)/shard_map/ppermute | solution.py:252
  49.4 3.0 collective-permute-start.6
  58.8 13.5 %collective-permute-done.6 = bf16[259,256]{1,0:T(8,128)(2,1)S(1)} collective-permute-done((bf16[259,256]{1,0:T(8,128)(2,1)S(1)}, bf16[259,256]{1,0:T(8,128)(2,1)S(1)}, u32[]{:S(2)}, u32[]{:S(2)}) %collective-permute-start.6) | collective-permute-done | bytes 132640 | tf_op jit(solution)/shard_map/ppermute | solution.py:252
  83.2 2.8 collective-permute-start.22
  89.0 6.7 %all_gather.3 = bf16[256,1024]{1,0:T(8,128)(2,1)S(1)} all-gather(bf16[64,1024]{1,0:T(8,128)(2,1)S(1)} %bitcast.247), channel_id=1, replica_groups=mesh['ctx'=8,'tp'=4] {'tp'}, dimensions={0}, use_global_device_ids=true | all-gather | bytes 655360 | tf_op jit(solution)/shard_map/all_gather | solution.py:348
  95.7 2.4 fusion.71
  98.2 6.3 %fusion.65 = (f32[8,128,2048]{2,1,0:T(8,128)}, f32[8,128,2048]{2,1,0:T(8,128)}) fusion(f32[8,128,4096]{2,1,0:T(8,128)S(1)} %bitcast.236), kind=kLoop, calls=%fused_computation.171 | loop fusion | bytes 33554432 | tf_op jit(solution)/shard_map/slice | solution.py:183
  104.5 2.4 collective-permute-start.25
  106.8 2.9 collective-permute-start.26
  109.8 2.1 fusion.31
  114.3 2.1 fusion.30
  129.1 2.0 collective-permute-done.16
  134.5 7.2 %collective-permute-done.19 = bf16[128,2048]{1,0:T(8,128)(2,1)S(1)} collective-permute-done((bf16[128,2048]{1,0:T(8,128)(2,1)S(1)}, bf16[128,2048]{1,0:T(8,128)(2,1)S(1)}, u32[]{:S(2)}, u32[]{:S(2)}) %collective-permute-start.19) | collective-permute-done | bytes 524320 | tf_op jit(solution)/shard_map/ppermute | solution.py:198
  141.8 2.1 bitcast_add_fusion.24
  143.9 2.8 collective-permute-done.17
  146.7 2.1 bitcast_add_fusion.26
  169.9 1.8 collective-permute-start.35
  171.7 11.3 %collective-permute-done.29 = bf16[128,2048]{1,0:T(8,128)(2,1)S(1)} collective-permute-done((bf16[128,2048]{1,0:T(8,128)(2,1)}, bf16[128,2048]{1,0:T(8,128)(2,1)S(1)}, u32[]{:S(2)}, u32[]{:S(2)}) %collective-permute-start.29) | collective-permute-done | bytes 524320 | tf_op jit(solution)/shard_map/ppermute | solution.py:197
  186.1 1.8 collective-permute-start.36
  187.9 10.6 %collective-permute-done.30 = bf16[128,2048]{1,0:T(8,128)(2,1)S(1)} collective-permute-done((bf16[128,2048]{1,0:T(8,128)(2,1)S(1)}, bf16[128,2048]{1,0:T(8,128)(2,1)S(1)}, u32[]{:S(2)}, u32[]{:S(2)}) %collective-permute-start.30) | collective-permute-done | bytes 524320 | tf_op jit(solution)/shard_map/ppermute | solution.py:197
  200.2 2.3 fusion.19
  204.2 8.8 %collective-permute-done.31 = bf16[128,2048]{1,0:T(8,128)(2,1)S(1)} collective-permute-done((bf16[128,2048]{1,0:T(8,128)(2,1)S(1)}, bf16[128,2048]{1,0:T(8,128)(2,1)S(1)}, u32[]{:S(2)}, u32[]{:S(2)}) %collective-permute-start.31) | collective-permute-done | bytes 524320 | tf_op jit(solution)/shard_map/ppermute | solution.py:197
  213.1 2.1 fusion.23
  220.5 7.4 %collective-permute-done.32 = bf16[128,2048]{1,0:T(8,128)(2,1)} collective-permute-done((bf16[128,2048]{1,0:T(8,128)(2,1)}, bf16[128,2048]{1,0:T(8,128)(2,1)}, u32[]{:S(2)}, u32[]{:S(2)}) %collective-permute-start.32) | collective-permute-done | bytes 524320 | tf_op jit(solution)/shard_map/ppermute | solution.py:197
  229.7 2.9 fusion.73
  234.0 6.9 %collective-permute-done.33 = bf16[128,2048]{1,0:T(8,128)(2,1)S(1)} collective-permute-done((bf16[128,2048]{1,0:T(8,128)(2,1)S(1)}, bf16[128,2048]{1,0:T(8,128)(2,1)S(1)}, u32[]{:S(2)}, u32[]{:S(2)}) %collective-permute-start.33) | collective-permute-done | bytes 524320 | tf_op jit(solution)/shard_map/ppermute | solution.py:197
  242.2 8.1 %fusion.64 = (f32[8,160,2048]{2,1,0:T(8,128)}, f32[8,160,2048]{2,1,0:T(8,128)}) fusion(f32[8,160,4096]{2,1,0:T(8,128)S(1)} %bitcast.235), kind=kLoop, calls=%fused_computation.170 | loop fusion | bytes 41943040 | tf_op jit(solution)/shard_map/slice | solution.py:108
  252.2 1.8 fusion.29
  254.0 1.9 collective-permute-start.46
  255.9 9.4 %collective-permute-done.39 = bf16[160,2048]{1,0:T(8,128)(2,1)S(1)} collective-permute-done((bf16[160,2048]{1,0:T(8,128)(2,1)S(1)}, bf16[160,2048]{1,0:T(8,128)(2,1)S(1)}, u32[]{:S(2)}, u32[]{:S(2)}) %collective-permute-start.39) | collective-permute-done | bytes 655392 | tf_op jit(solution)/shard_map/ppermute | solution.py:119
  268.7 1.9 collective-permute-start.47
  270.6 9.5 %collective-permute-done.40 = bf16[160,2048]{1,0:T(8,128)(2,1)S(1)} collective-permute-done((bf16[160,2048]{1,0:T(8,128)(2,1)S(1)}, bf16[160,2048]{1,0:T(8,128)(2,1)S(1)}, u32[]{:S(2)}, u32[]{:S(2)}) %collective-permute-start.40) | collective-permute-done | bytes 655392 | tf_op jit(solution)/shard_map/ppermute | solution.py:119
  283.6 1.9 collective-permute-start.48
  285.5 9.5 %collective-permute-done.41 = bf16[160,2048]{1,0:T(8,128)(2,1)S(1)} collective-permute-done((bf16[160,2048]{1,0:T(8,128)(2,1)S(1)}, bf16[160,2048]{1,0:T(8,128)(2,1)S(1)}, u32[]{:S(2)}, u32[]{:S(2)}) %collective-permute-start.41) | collective-permute-done | bytes 655392 | tf_op jit(solution)/shard_map/ppermute | solution.py:119
  298.5 1.9 collective-permute-start.49
  300.4 9.5 %collective-permute-done.42 = bf16[160,2048]{1,0:T(8,128)(2,1)S(1)} collective-permute-done((bf16[160,2048]{1,0:T(8,128)(2,1)S(1)}, bf16[160,2048]{1,0:T(8,128)(2,1)S(1)}, u32[]{:S(2)}, u32[]{:S(2)}) %collective-permute-start.42) | collective-permute-done | bytes 655392 | tf_op jit(solution)/shard_map/ppermute | solution.py:119
  313.1 2.3 collective-permute-start.50
  315.3 7.6 %convolution_convert_fusion = bf16[256,4096]{1,0:T(8,128)(2,1)} fusion(bf16[256,1024]{1,0:T(8,128)(2,1)S(1)} %all_gather.3, bf16[1024,4096]{1,0:T(8,128)(2,1)} %param.14), kind=kOutput, calls=%fused_computation.3 | convolution fusion | flops 2148532224 | bytes 11010048 | tf_op jit(solution)/shard_map/dot_general | solution.py:349
  323.0 2.8 collective-permute-done.43
  329.0 2.1 collective-permute-start.51
  331.1 4.1 %convolution_convert_fusion.1 = bf16[256,4096]{1,0:T(8,128)(2,1)} fusion(bf16[256,1280]{1,0:T(8,128)(2,1)S(1)} %concatenate.45, bf16[1280,4096]{1,0:T(8,128)(2,1)S(1)} %bitcast.254), kind=kOutput, calls=%fused_computation.4 | convolution fusion | flops 2685403136 | bytes 13238272 | tf_op jit(solution)/shard_map/dot_general | solution.py:375
  335.2 7.3 %collective-permute-done.44 = bf16[160,2048]{1,0:T(8,128)(2,1)S(1)} collective-permute-done((bf16[160,2048]{1,0:T(8,128)(2,1)S(1)}, bf16[160,2048]{1,0:T(8,128)(2,1)S(1)}, u32[]{:S(2)}, u32[]{:S(2)}) %collective-permute-start.44) | collective-permute-done | bytes 655392 | tf_op jit(solution)/shard_map/ppermute | solution.py:119
  345.4 2.2 collective-permute-start.52
  349.1 5.6 %collective-permute-done.45 = bf16[160,2048]{1,0:T(8,128)(2,1)S(1)} collective-permute-done((bf16[160,2048]{1,0:T(8,128)(2,1)S(1)}, bf16[160,2048]{1,0:T(8,128)(2,1)S(1)}, u32[]{:S(2)}, u32[]{:S(2)}) %collective-permute-start.45) | collective-permute-done | bytes 655392 | tf_op jit(solution)/shard_map/ppermute | solution.py:119
  (207 shorter events, 90.7 us)
Async XLA Ops:
  9.1 25.8 %collective-permute-start = (f32[256,1280]{1,0:T(8,128)S(1)}, f32[256,1280]{1,0:T(8,128)}, u32[]{:S(2)}, u32[]{:S(2)}) collective-permute-start(f32[256,1280]{1,0:T(8,128)S(1)} %fusion.70), channel_id=1, source_target_pairs={{0,1},{1,0},{2,3},{3,2},{4,5},{5,4},{6,7},{7,6},{8,9},{9,8},{10,11... | collective-permute-start | bytes 3932168 | tf_op jit(solution)/shard_map/ppermute | solution.py:215
  17.6 19.0 %collective-permute-start.11 = (bf16[128,1024]{1,0:T(8,128)(2,1)}, bf16[128,1024]{1,0:T(8,128)(2,1)}, u32[]{:S(2)}, u32[]{:S(2)}) collective-permute-start(bf16[128,1024]{1,0:T(8,128)(2,1)} %constant_dynamic-slice_fusion), channel_id=1, source_target_pairs={{0,2},{1,3},{2,0},{3,1},{4,6},{5,7},{6,4},{7,5},{8,10},{9,11},{10,... | collective-permute-start | bytes 786440 | tf_op jit(solution)/shard_map/ppermute | solution.py:238
  42.5 10.6 %collective-permute-start.10 = (f32[64,1024]{1,0:T(8,128)S(1)}, f32[64,1024]{1,0:T(8,128)S(1)}, u32[]{:S(2)}, u32[]{:S(2)}) collective-permute-start(f32[64,1024]{1,0:T(8,128)S(1)} %constant_dynamic-slice_fusion.3), channel_id=1, source_target_pairs={{0,2},{1,3},{2,0},{3,1},{4,6},{5,7},{6,4},{7,5},{8,10},{9,11},{10,... | collective-permute-start | bytes 786440 | tf_op jit(solution)/shard_map/ppermute | solution.py:221
  44.3 9.8 %collective-permute-start.3 = (bf16[259,256]{1,0:T(8,128)(2,1)S(1)}, bf16[259,256]{1,0:T(8,128)(2,1)S(1)}, u32[]{:S(2)}, u32[]{:S(2)}) collective-permute-start(bf16[259,256]{1,0:T(8,128)(2,1)S(1)} %get-tuple-element.19), channel_id=1, source_target_pairs={{0,28},{4,0},{8,4},{12,8},{16,12},{20,16},{24,20},{28,24},{1,29},{... | collective-permute-start | bytes 397832 | tf_op jit(solution)/shard_map/ppermute | solution.py:252
  49.4 9.4 %collective-permute-start.5 = (bf16[259,256]{1,0:T(8,128)(2,1)S(1)}, bf16[259,256]{1,0:T(8,128)(2,1)S(1)}, u32[]{:S(2)}, u32[]{:S(2)}) collective-permute-start(bf16[259,256]{1,0:T(8,128)(2,1)S(1)} %get-tuple-element.19), channel_id=1, source_target_pairs={{0,20},{4,24},{8,28},{12,0},{16,4},{20,8},{24,12},{28,16},{1,21},{... | collective-permute-start | bytes 397832 | tf_op jit(solution)/shard_map/ppermute | solution.py:252
  49.4 22.9 %collective-permute-start.6 = (bf16[259,256]{1,0:T(8,128)(2,1)S(1)}, bf16[259,256]{1,0:T(8,128)(2,1)S(1)}, u32[]{:S(2)}, u32[]{:S(2)}) collective-permute-start(bf16[259,256]{1,0:T(8,128)(2,1)S(1)} %get-tuple-element.19), channel_id=1, source_target_pairs={{0,16},{4,20},{8,24},{12,28},{16,0},{20,4},{24,8},{28,12},{1,17},{... | collective-permute-start | bytes 397832 | tf_op jit(solution)/shard_map/ppermute | solution.py:252
  53.0 20.7 %collective-permute-start.7 = (bf16[259,256]{1,0:T(8,128)(2,1)S(1)}, bf16[259,256]{1,0:T(8,128)(2,1)S(1)}, u32[]{:S(2)}, u32[]{:S(2)}) collective-permute-start(bf16[259,256]{1,0:T(8,128)(2,1)S(1)} %get-tuple-element.19), channel_id=1, source_target_pairs={{0,12},{4,16},{8,20},{12,24},{16,28},{20,0},{24,4},{28,8},{1,13},{... | collective-permute-start | bytes 397832 | tf_op jit(solution)/shard_map/ppermute | solution.py:252
  54.2 19.6 %collective-permute-start.8 = (bf16[259,256]{1,0:T(8,128)(2,1)S(1)}, bf16[259,256]{1,0:T(8,128)(2,1)S(1)}, u32[]{:S(2)}, u32[]{:S(2)}) collective-permute-start(bf16[259,256]{1,0:T(8,128)(2,1)S(1)} %get-tuple-element.19), channel_id=1, source_target_pairs={{0,8},{4,12},{8,16},{12,20},{16,24},{20,28},{24,0},{28,4},{1,9},{5... | collective-permute-start | bytes 397832 | tf_op jit(solution)/shard_map/ppermute | solution.py:252
  55.9 17.9 %collective-permute-start.9 = (bf16[259,256]{1,0:T(8,128)(2,1)S(1)}, bf16[259,256]{1,0:T(8,128)(2,1)S(1)}, u32[]{:S(2)}, u32[]{:S(2)}) collective-permute-start(bf16[259,256]{1,0:T(8,128)(2,1)S(1)} %get-tuple-element.19), channel_id=1, source_target_pairs={{0,4},{4,8},{8,12},{12,16},{16,20},{20,24},{24,28},{28,0},{1,5},{5... | collective-permute-start | bytes 397832 | tf_op jit(solution)/shard_map/ppermute | solution.py:252
  82.3 22.2 %collective-permute-start.20 = (bf16[256,256]{1,0:T(8,128)(2,1)}, bf16[256,256]{1,0:T(8,128)(2,1)}, u32[]{:S(2)}, u32[]{:S(2)}) collective-permute-start(bf16[256,256]{1,0:T(8,128)(2,1)} %get-tuple-element.30), channel_id=1, source_target_pairs={{0,4},{4,8},{8,12},{12,16},{16,20},{20,24},{24,28},{28,0},{1,5},{5... | collective-permute-start | bytes 393224 | tf_op jit(solution)/shard_map/ppermute | solution.py:263
  82.3 24.6 %collective-permute-start.21 = (bf16[256,256]{1,0:T(8,128)(2,1)}, bf16[256,256]{1,0:T(8,128)(2,1)}, u32[]{:S(2)}, u32[]{:S(2)}) collective-permute-start(bf16[256,256]{1,0:T(8,128)(2,1)} %get-tuple-element.36), channel_id=1, source_target_pairs={{0,8},{4,12},{8,16},{12,20},{16,24},{20,28},{24,0},{28,4},{1,9},{5... | collective-permute-start | bytes 393224 | tf_op jit(solution)/shard_map/ppermute | solution.py:263
  83.2 28.7 %collective-permute-start.22 = (bf16[256,256]{1,0:T(8,128)(2,1)}, bf16[256,256]{1,0:T(8,128)(2,1)}, u32[]{:S(2)}, u32[]{:S(2)}) collective-permute-start(bf16[256,256]{1,0:T(8,128)(2,1)} %get-tuple-element.35), channel_id=1, source_target_pairs={{0,12},{4,16},{8,20},{12,24},{16,28},{20,0},{24,4},{28,8},{1,13},{... | collective-permute-start | bytes 393224 | tf_op jit(solution)/shard_map/ppermute | solution.py:263
  86.0 25.9 %collective-permute-start.23 = (bf16[256,256]{1,0:T(8,128)(2,1)}, bf16[256,256]{1,0:T(8,128)(2,1)}, u32[]{:S(2)}, u32[]{:S(2)}) collective-permute-start(bf16[256,256]{1,0:T(8,128)(2,1)} %get-tuple-element.34), channel_id=1, source_target_pairs={{0,16},{4,20},{8,24},{12,28},{16,0},{20,4},{24,8},{28,12},{1,17},{... | collective-permute-start | bytes 393224 | tf_op jit(solution)/shard_map/ppermute | solution.py:263
  87.6 24.3 %collective-permute-start.24 = (bf16[256,256]{1,0:T(8,128)(2,1)}, bf16[256,256]{1,0:T(8,128)(2,1)}, u32[]{:S(2)}, u32[]{:S(2)}) collective-permute-start(bf16[256,256]{1,0:T(8,128)(2,1)} %get-tuple-element.33), channel_id=1, source_target_pairs={{0,20},{4,24},{8,28},{12,0},{16,4},{20,8},{24,12},{28,16},{1,21},{... | collective-permute-start | bytes 393224 | tf_op jit(solution)/shard_map/ppermute | solution.py:263
  104.5 7.4 %collective-permute-start.25 = (bf16[256,256]{1,0:T(8,128)(2,1)S(1)}, bf16[256,256]{1,0:T(8,128)(2,1)S(1)}, u32[]{:S(2)}, u32[]{:S(2)}) collective-permute-start(bf16[256,256]{1,0:T(8,128)(2,1)S(1)} %get-tuple-element.32), channel_id=1, source_target_pairs={{0,24},{4,28},{8,0},{12,4},{16,8},{20,12},{24,16},{28,20},{1,25},{... | collective-permute-start | bytes 393224 | tf_op jit(solution)/shard_map/ppermute | solution.py:263
  111.9 14.6 %collective-permute-start.18 = (bf16[128,2048]{1,0:T(8,128)(2,1)}, bf16[128,2048]{1,0:T(8,128)(2,1)}, u32[]{:S(2)}, u32[]{:S(2)}) collective-permute-start(bf16[128,2048]{1,0:T(8,128)(2,1)} %fusion.31), channel_id=1, source_target_pairs={{0,4},{8,0},{16,8},{24,16},{28,24},{20,28},{12,20},{4,12},{1,5},{9... | collective-permute-start | bytes 1572872 | tf_op jit(solution)/shard_map/ppermute | solution.py:198
  114.2 10.2 %collective-permute-start.27 = (f32[256,256]{1,0:T(8,128)S(1)}, f32[256,256]{1,0:T(8,128)}, u32[]{:S(2)}, u32[]{:S(2)}) collective-permute-start(f32[256,256]{1,0:T(8,128)S(1)} %fusion.39), channel_id=1, source_target_pairs={{0,1},{1,0},{2,3},{3,2},{4,5},{5,4},{6,7},{7,6},{8,9},{9,8},{10,11... | collective-permute-start | bytes 786440 | tf_op jit(solution)/shard_map/ppermute | solution.py:274
  116.4 14.6 %collective-permute-start.16 = (bf16[128,2048]{1,0:T(8,128)(2,1)}, bf16[128,2048]{1,0:T(8,128)(2,1)}, u32[]{:S(2)}, u32[]{:S(2)}) collective-permute-start(bf16[128,2048]{1,0:T(8,128)(2,1)} %fusion.30), channel_id=1, source_target_pairs={{0,8},{8,16},{16,24},{24,28},{28,20},{20,12},{12,4},{4,0},{1,9},{9... | collective-permute-start | bytes 1572872 | tf_op jit(solution)/shard_map/ppermute | solution.py:197
  125.4 9.1 %collective-permute-start.28 = (f32[256,256]{1,0:T(8,128)S(1)}, f32[256,256]{1,0:T(8,128)S(1)}, u32[]{:S(2)}, u32[]{:S(2)}) collective-permute-start(f32[256,256]{1,0:T(8,128)S(1)} %add.720), channel_id=1, source_target_pairs={{0,2},{1,3},{2,0},{3,1},{4,6},{5,7},{6,4},{7,5},{8,10},{9,11},{10,... | collective-permute-start | bytes 786440 | tf_op jit(solution)/shard_map/ppermute | solution.py:274
  128.0 13.8 %collective-permute-start.19 = (bf16[128,2048]{1,0:T(8,128)(2,1)S(1)}, bf16[128,2048]{1,0:T(8,128)(2,1)S(1)}, u32[]{:S(2)}, u32[]{:S(2)}) collective-permute-start(bf16[128,2048]{1,0:T(8,128)(2,1)S(1)} %fusion.26), channel_id=1, source_target_pairs={{0,4},{8,0},{16,8},{24,16},{28,24},{20,28},{12,20},{4,12},{1,5},{9... | collective-permute-start | bytes 1572872 | tf_op jit(solution)/shard_map/ppermute | solution.py:198
  132.5 14.3 %collective-permute-start.17 = (bf16[128,2048]{1,0:T(8,128)(2,1)S(1)}, bf16[128,2048]{1,0:T(8,128)(2,1)S(1)}, u32[]{:S(2)}, u32[]{:S(2)}) collective-permute-start(bf16[128,2048]{1,0:T(8,128)(2,1)S(1)} %fusion.27), channel_id=1, source_target_pairs={{0,8},{8,16},{16,24},{24,28},{28,20},{20,12},{12,4},{4,0},{1,9},{9... | collective-permute-start | bytes 1572872 | tf_op jit(solution)/shard_map/ppermute | solution.py:197
  148.9 19.6 %collective-permute-start.34 = (bf16[128,2048]{1,0:T(8,128)(2,1)}, bf16[128,2048]{1,0:T(8,128)(2,1)}, u32[]{:S(2)}, u32[]{:S(2)}) collective-permute-start(bf16[128,2048]{1,0:T(8,128)(2,1)} %bitcast_add_fusion.24), channel_id=1, source_target_pairs={{0,4},{8,0},{16,8},{24,16},{28,24},{20,28},{12,20},{4,12},{1,5},{9... | collective-permute-start | bytes 1572872 | tf_op jit(solution)/shard_map/ppermute | solution.py:198
  150.9 17.1 %collective-permute-start.13 = (bf16[64,1024]{1,0:T(8,128)(2,1)S(1)}, bf16[64,1024]{1,0:T(8,128)(2,1)S(1)}, u32[]{:S(2)}, u32[]{:S(2)}) collective-permute-start(bf16[64,1024]{1,0:T(8,128)(2,1)S(1)} %copy_bitcast_fusion.1), channel_id=1, source_target_pairs={{0,1},{1,2},{2,3},{3,0},{4,5},{5,6},{6,7},{7,4},{8,9},{9,10},{10,1... | collective-permute-start | bytes 393224 | tf_op jit(solution)/shard_map/ppermute | solution.py:23
  166.1 18.6 %collective-permute-start.14 = (bf16[64,1024]{1,0:T(8,128)(2,1)S(1)}, bf16[64,1024]{1,0:T(8,128)(2,1)S(1)}, u32[]{:S(2)}, u32[]{:S(2)}) collective-permute-start(bf16[64,1024]{1,0:T(8,128)(2,1)S(1)} %copy_bitcast_fusion.1), channel_id=1, source_target_pairs={{0,3},{1,0},{2,1},{3,2},{4,7},{5,4},{6,5},{7,6},{8,11},{9,8},{10,9... | collective-permute-start | bytes 393224 | tf_op jit(solution)/shard_map/ppermute | solution.py:32
  168.0 32.1 %collective-permute-start.15 = (bf16[64,1024]{1,0:T(8,128)(2,1)S(1)}, bf16[64,1024]{1,0:T(8,128)(2,1)S(1)}, u32[]{:S(2)}, u32[]{:S(2)}) collective-permute-start(bf16[64,1024]{1,0:T(8,128)(2,1)S(1)} %collective-permute-done.13), channel_id=1, source_target_pairs={{0,1},{1,2},{2,3},{3,0},{4,5},{5,6},{6,7},{7,4},{8,9},{9,10},{10,1... | collective-permute-start | bytes 393224 | tf_op jit(solution)/shard_map/ppermute | solution.py:23
  168.1 15.0 %collective-permute-start.29 = (bf16[128,2048]{1,0:T(8,128)(2,1)}, bf16[128,2048]{1,0:T(8,128)(2,1)S(1)}, u32[]{:S(2)}, u32[]{:S(2)}) collective-permute-start(bf16[128,2048]{1,0:T(8,128)(2,1)} %bitcast_add_fusion.26), channel_id=1, source_target_pairs={{0,8},{8,16},{16,24},{24,28},{28,20},{20,12},{12,4},{4,0},{1,9},{9... | collective-permute-start | bytes 1572872 | tf_op jit(solution)/shard_map/ppermute | solution.py:197
  169.9 14.8 %collective-permute-start.35 = (bf16[128,2048]{1,0:T(8,128)(2,1)S(1)}, bf16[128,2048]{1,0:T(8,128)(2,1)S(1)}, u32[]{:S(2)}, u32[]{:S(2)}) collective-permute-start(bf16[128,2048]{1,0:T(8,128)(2,1)S(1)} %fusion.21), channel_id=1, source_target_pairs={{0,4},{8,0},{16,8},{24,16},{28,24},{20,28},{12,20},{4,12},{1,5},{9... | collective-permute-start | bytes 1572872 | tf_op jit(solution)/shard_map/ppermute | solution.py:198
  184.4 14.1 %collective-permute-start.30 = (bf16[128,2048]{1,0:T(8,128)(2,1)S(1)}, bf16[128,2048]{1,0:T(8,128)(2,1)S(1)}, u32[]{:S(2)}, u32[]{:S(2)}) collective-permute-start(bf16[128,2048]{1,0:T(8,128)(2,1)S(1)} %fusion.25), channel_id=1, source_target_pairs={{0,8},{8,16},{16,24},{24,28},{28,20},{20,12},{12,4},{4,0},{1,9},{9... | collective-permute-start | bytes 1572872 | tf_op jit(solution)/shard_map/ppermute | solution.py:197
  186.1 14.1 %collective-permute-start.36 = (bf16[128,2048]{1,0:T(8,128)(2,1)S(1)}, bf16[128,2048]{1,0:T(8,128)(2,1)S(1)}, u32[]{:S(2)}, u32[]{:S(2)}) collective-permute-start(bf16[128,2048]{1,0:T(8,128)(2,1)S(1)} %fusion.20), channel_id=1, source_target_pairs={{0,4},{8,0},{16,8},{24,16},{28,24},{20,28},{12,20},{4,12},{1,5},{9... | collective-permute-start | bytes 1572872 | tf_op jit(solution)/shard_map/ppermute | solution.py:198
  199.8 13.3 %collective-permute-start.31 = (bf16[128,2048]{1,0:T(8,128)(2,1)S(1)}, bf16[128,2048]{1,0:T(8,128)(2,1)S(1)}, u32[]{:S(2)}, u32[]{:S(2)}) collective-permute-start(bf16[128,2048]{1,0:T(8,128)(2,1)S(1)} %fusion.24), channel_id=1, source_target_pairs={{0,8},{8,16},{16,24},{24,28},{28,20},{20,12},{12,4},{4,0},{1,9},{9... | collective-permute-start | bytes 1572872 | tf_op jit(solution)/shard_map/ppermute | solution.py:197
  202.5 14.8 %collective-permute-start.37 = (bf16[128,2048]{1,0:T(8,128)(2,1)}, bf16[128,2048]{1,0:T(8,128)(2,1)}, u32[]{:S(2)}, u32[]{:S(2)}) collective-permute-start(bf16[128,2048]{1,0:T(8,128)(2,1)} %fusion.19), channel_id=1, source_target_pairs={{0,4},{8,0},{16,8},{24,16},{28,24},{20,28},{12,20},{4,12},{1,5},{9... | collective-permute-start | bytes 1572872 | tf_op jit(solution)/shard_map/ppermute | solution.py:198
  215.2 12.7 %collective-permute-start.32 = (bf16[128,2048]{1,0:T(8,128)(2,1)}, bf16[128,2048]{1,0:T(8,128)(2,1)}, u32[]{:S(2)}, u32[]{:S(2)}) collective-permute-start(bf16[128,2048]{1,0:T(8,128)(2,1)} %fusion.23), channel_id=1, source_target_pairs={{0,8},{8,16},{16,24},{24,28},{28,20},{20,12},{12,4},{4,0},{1,9},{9... | collective-permute-start | bytes 1572872 | tf_op jit(solution)/shard_map/ppermute | solution.py:197
  218.7 13.9 %collective-permute-start.38 = (bf16[128,2048]{1,0:T(8,128)(2,1)S(1)}, bf16[128,2048]{1,0:T(8,128)(2,1)S(1)}, u32[]{:S(2)}, u32[]{:S(2)}) collective-permute-start(bf16[128,2048]{1,0:T(8,128)(2,1)S(1)} %fusion.18), channel_id=1, source_target_pairs={{0,4},{8,0},{16,8},{24,16},{28,24},{20,28},{12,20},{4,12},{1,5},{9... | collective-permute-start | bytes 1572872 | tf_op jit(solution)/shard_map/ppermute | solution.py:198
  229.4 11.5 %collective-permute-start.33 = (bf16[128,2048]{1,0:T(8,128)(2,1)S(1)}, bf16[128,2048]{1,0:T(8,128)(2,1)S(1)}, u32[]{:S(2)}, u32[]{:S(2)}) collective-permute-start(bf16[128,2048]{1,0:T(8,128)(2,1)S(1)} %fusion.22), channel_id=1, source_target_pairs={{0,8},{8,16},{16,24},{24,28},{28,20},{20,12},{12,4},{4,0},{1,9},{9... | collective-permute-start | bytes 1572872 | tf_op jit(solution)/shard_map/ppermute | solution.py:197
  251.8 13.4 %collective-permute-start.39 = (bf16[160,2048]{1,0:T(8,128)(2,1)S(1)}, bf16[160,2048]{1,0:T(8,128)(2,1)S(1)}, u32[]{:S(2)}, u32[]{:S(2)}) collective-permute-start(bf16[160,2048]{1,0:T(8,128)(2,1)S(1)} %fusion.28), channel_id=1, source_target_pairs={{0,8},{8,16},{16,24},{24,28},{28,20},{20,12},{12,4},{4,0},{1,9},{9... | collective-permute-start | bytes 1966088 | tf_op jit(solution)/shard_map/ppermute | solution.py:119
  254.0 13.2 %collective-permute-start.46 = (bf16[160,2048]{1,0:T(8,128)(2,1)S(1)}, bf16[160,2048]{1,0:T(8,128)(2,1)S(1)}, u32[]{:S(2)}, u32[]{:S(2)}) collective-permute-start(bf16[160,2048]{1,0:T(8,128)(2,1)S(1)} %fusion.29), channel_id=1, source_target_pairs={{0,4},{8,0},{16,8},{24,16},{28,24},{20,28},{12,20},{4,12},{1,5},{9... | collective-permute-start | bytes 1966088 | tf_op jit(solution)/shard_map/ppermute | solution.py:120
  266.7 13.4 %collective-permute-start.40 = (bf16[160,2048]{1,0:T(8,128)(2,1)S(1)}, bf16[160,2048]{1,0:T(8,128)(2,1)S(1)}, u32[]{:S(2)}, u32[]{:S(2)}) collective-permute-start(bf16[160,2048]{1,0:T(8,128)(2,1)S(1)} %fusion.16), channel_id=1, source_target_pairs={{0,8},{8,16},{16,24},{24,28},{28,20},{20,12},{12,4},{4,0},{1,9},{9... | collective-permute-start | bytes 1966088 | tf_op jit(solution)/shard_map/ppermute | solution.py:119
  268.7 14.7 %collective-permute-start.47 = (bf16[160,2048]{1,0:T(8,128)(2,1)S(1)}, bf16[160,2048]{1,0:T(8,128)(2,1)S(1)}, u32[]{:S(2)}, u32[]{:S(2)}) collective-permute-start(bf16[160,2048]{1,0:T(8,128)(2,1)S(1)} %fusion.10), channel_id=1, source_target_pairs={{0,4},{8,0},{16,8},{24,16},{28,24},{20,28},{12,20},{4,12},{1,5},{9... | collective-permute-start | bytes 1966088 | tf_op jit(solution)/shard_map/ppermute | solution.py:120
  281.6 13.4 %collective-permute-start.41 = (bf16[160,2048]{1,0:T(8,128)(2,1)S(1)}, bf16[160,2048]{1,0:T(8,128)(2,1)S(1)}, u32[]{:S(2)}, u32[]{:S(2)}) collective-permute-start(bf16[160,2048]{1,0:T(8,128)(2,1)S(1)} %fusion.15), channel_id=1, source_target_pairs={{0,8},{8,16},{16,24},{24,28},{28,20},{20,12},{12,4},{4,0},{1,9},{9... | collective-permute-start | bytes 1966088 | tf_op jit(solution)/shard_map/ppermute | solution.py:119
  283.6 14.7 %collective-permute-start.48 = (bf16[160,2048]{1,0:T(8,128)(2,1)S(1)}, bf16[160,2048]{1,0:T(8,128)(2,1)S(1)}, u32[]{:S(2)}, u32[]{:S(2)}) collective-permute-start(bf16[160,2048]{1,0:T(8,128)(2,1)S(1)} %fusion.9), channel_id=1, source_target_pairs={{0,4},{8,0},{16,8},{24,16},{28,24},{20,28},{12,20},{4,12},{1,5},{9... | collective-permute-start | bytes 1966088 | tf_op jit(solution)/shard_map/ppermute | solution.py:120
  296.5 13.4 %collective-permute-start.42 = (bf16[160,2048]{1,0:T(8,128)(2,1)S(1)}, bf16[160,2048]{1,0:T(8,128)(2,1)S(1)}, u32[]{:S(2)}, u32[]{:S(2)}) collective-permute-start(bf16[160,2048]{1,0:T(8,128)(2,1)S(1)} %fusion.14), channel_id=1, source_target_pairs={{0,8},{8,16},{16,24},{24,28},{28,20},{20,12},{12,4},{4,0},{1,9},{9... | collective-permute-start | bytes 1966088 | tf_op jit(solution)/shard_map/ppermute | solution.py:119
  298.5 14.4 %collective-permute-start.49 = (bf16[160,2048]{1,0:T(8,128)(2,1)S(1)}, bf16[160,2048]{1,0:T(8,128)(2,1)S(1)}, u32[]{:S(2)}, u32[]{:S(2)}) collective-permute-start(bf16[160,2048]{1,0:T(8,128)(2,1)S(1)} %fusion.8), channel_id=1, source_target_pairs={{0,4},{8,0},{16,8},{24,16},{28,24},{20,28},{12,20},{4,12},{1,5},{9... | collective-permute-start | bytes 1966088 | tf_op jit(solution)/shard_map/ppermute | solution.py:120
  311.4 14.3 %collective-permute-start.43 = (bf16[160,2048]{1,0:T(8,128)(2,1)S(1)}, bf16[160,2048]{1,0:T(8,128)(2,1)S(1)}, u32[]{:S(2)}, u32[]{:S(2)}) collective-permute-start(bf16[160,2048]{1,0:T(8,128)(2,1)S(1)} %fusion.13), channel_id=1, source_target_pairs={{0,8},{8,16},{16,24},{24,28},{28,20},{20,12},{12,4},{4,0},{1,9},{9... | collective-permute-start | bytes 1966088 | tf_op jit(solution)/shard_map/ppermute | solution.py:119
  313.1 15.7 %collective-permute-start.50 = (bf16[160,2048]{1,0:T(8,128)(2,1)S(1)}, bf16[160,2048]{1,0:T(8,128)(2,1)S(1)}, u32[]{:S(2)}, u32[]{:S(2)}) collective-permute-start(bf16[160,2048]{1,0:T(8,128)(2,1)S(1)} %fusion.7), channel_id=1, source_target_pairs={{0,4},{8,0},{16,8},{24,16},{28,24},{20,28},{12,20},{4,12},{1,5},{9... | collective-permute-start | bytes 1966088 | tf_op jit(solution)/shard_map/ppermute | solution.py:120
  327.2 15.3 %collective-permute-start.44 = (bf16[160,2048]{1,0:T(8,128)(2,1)S(1)}, bf16[160,2048]{1,0:T(8,128)(2,1)S(1)}, u32[]{:S(2)}, u32[]{:S(2)}) collective-permute-start(bf16[160,2048]{1,0:T(8,128)(2,1)S(1)} %fusion.12), channel_id=1, source_target_pairs={{0,8},{8,16},{16,24},{24,28},{28,20},{20,12},{12,4},{4,0},{1,9},{9... | collective-permute-start | bytes 1966088 | tf_op jit(solution)/shard_map/ppermute | solution.py:119
  329.0 16.3 %collective-permute-start.51 = (bf16[160,2048]{1,0:T(8,128)(2,1)S(1)}, bf16[160,2048]{1,0:T(8,128)(2,1)S(1)}, u32[]{:S(2)}, u32[]{:S(2)}) collective-permute-start(bf16[160,2048]{1,0:T(8,128)(2,1)S(1)} %fusion.6), channel_id=1, source_target_pairs={{0,4},{8,0},{16,8},{24,16},{28,24},{20,28},{12,20},{4,12},{1,5},{9... | collective-permute-start | bytes 1966088 | tf_op jit(solution)/shard_map/ppermute | solution.py:120
  344.0 10.6 %collective-permute-start.45 = (bf16[160,2048]{1,0:T(8,128)(2,1)S(1)}, bf16[160,2048]{1,0:T(8,128)(2,1)S(1)}, u32[]{:S(2)}, u32[]{:S(2)}) collective-permute-start(bf16[160,2048]{1,0:T(8,128)(2,1)S(1)} %fusion.11), channel_id=1, source_target_pairs={{0,8},{8,16},{16,24},{24,28},{28,20},{20,12},{12,4},{4,0},{1,9},{9... | collective-permute-start | bytes 1966088 | tf_op jit(solution)/shard_map/ppermute | solution.py:119
  345.4 10.7 %collective-permute-start.52 = (bf16[160,2048]{1,0:T(8,128)(2,1)S(1)}, bf16[160,2048]{1,0:T(8,128)(2,1)S(1)}, u32[]{:S(2)}, u32[]{:S(2)}) collective-permute-start(bf16[160,2048]{1,0:T(8,128)(2,1)S(1)} %fusion.5), channel_id=1, source_target_pairs={{0,4},{8,0},{16,8},{24,16},{28,24},{20,28},{12,20},{4,12},{1,5},{9... | collective-permute-start | bytes 1966088 | tf_op jit(solution)/shard_map/ppermute | solution.py:120
  (24 other events, 247.3 us)
